TPU v7x, 512 devices: a whole 4x4x16 slice. The times are simulated.
512 devices in a mesh: day: 64 (over x, z_lo, core), pair: 8 (over y, z_hi).
Axes of the slice: x: 4, y: 4, z: 16 (z_hi: 2, z_lo: 8; z = z_hi * 8 + z_lo), core: 2. Of those that a mesh axis runs over, the one named last changes fastest.
Arguments:
- spectra: bfloat16 [256, 128, 1024], P('day', 'pair'), may hold values from -4 to 4
- pair_list: int32 [4096, 2], P('pair'), may hold values from 0 to 127, as said below
- mask: int32 [256, 128], P('day'), may hold values from 0 to 1
Outputs:
- linear_stack: float32 [401, 4096], P(None, ('pair', 'day'))
- weighted_stack: float32 [401, 4096], P(None, ('pair', 'day'))
Inputs may be any that keep to these rules, and one draw needn't show every extreme that they name: `pair_list`: the two stations of a pair differ.
All inputs are finite; a program needn't handle non-finite values.
Results may differ from a plain program's by a relative error of at most 0.0039.
Values may be sent and summed in bfloat16 or wider, within the bound.
No kernel may reach another device: no remote copies, remote signals or barrier semaphores. Data moves between devices by JAX's collectives and lax.ppermute only.
A program may use at most 64 MiB of HBM per device.

v0:
```python
import math

import jax
import jax.numpy as jnp
from jax import lax
from jax.sharding import PartitionSpec as P

F = 512
MAXLAG = 200
LAGS = 401


def lag_table():
    lag = jnp.arange(LAGS, dtype=jnp.int32) - MAXLAG
    freq = jnp.arange(F, dtype=jnp.int32)
    phase = jnp.mod(lag[:, None] * freq[None, :], 2 * F).astype(jnp.float32) * (math.pi / F)
    scale = 1.0 / math.sqrt(F)
    cosine = jnp.cos(phase) * scale
    sine = jnp.sin(phase) * scale
    upper = jnp.concatenate([cosine, -sine], 1)
    lower = jnp.concatenate([sine, cosine], 1)
    return jnp.concatenate([upper, lower], 0).astype(jnp.bfloat16)


def per_device(spectra, pair_list, mask):
    gathered = lax.all_gather(spectra, "pair", axis=1, tiled=True)
    station_count = gathered.shape[1]
    pair_rows = pair_list.shape[0]
    first = pair_list[:, 0]
    second = pair_list[:, 1]
    column = lax.broadcasted_iota(jnp.int32, (pair_rows, station_count), 1)
    pick_first = (first[:, None] == column).astype(jnp.float32)
    pick_second = (second[:, None] == column).astype(jnp.float32)
    mask_float = mask.astype(jnp.float32)
    weights = jnp.einsum("ds,ps->dp", mask_float, pick_first) * jnp.einsum(
        "ds,ps->dp", mask_float, pick_second
    )
    count_local = jnp.sum(weights, 0, keepdims=True)
    groups = lax.axis_size("day")
    owned = pair_rows // groups
    start = lax.axis_index("day") * owned
    table = lag_table()

    def one_day(carry, inputs):
        day_spec, weight = inputs
        left = jnp.take(day_spec, first, axis=0).astype(jnp.float32)
        right = jnp.take(day_spec, second, axis=0).astype(jnp.float32)
        half = left.shape[1] // 2
        left_re, left_im = (left[:, :half], left[:, half:])
        right_re, right_im = (right[:, :half], right[:, half:])
        cross_re = left_re * right_re + left_im * right_im
        cross_im = left_im * right_re - left_re * right_im
        cross = jnp.concatenate([cross_re, cross_im], 1).astype(jnp.bfloat16)
        analytic = lax.dot_general(
            table, cross, (((1,), (1,)), ((), ())), preferred_element_type=jnp.float32
        )
        trace = analytic[:LAGS]
        hilbert = analytic[LAGS:]
        amplitude = jnp.sqrt(trace * trace + hilbert * hilbert)
        inverse = 1.0 / jnp.maximum(amplitude, 0.5)
        lin_sum, real_sum, imag_sum = carry
        lin_sum = lin_sum + weight[None, :] * trace
        real_sum = real_sum + weight[None, :] * (trace * inverse)
        imag_sum = imag_sum + weight[None, :] * (hilbert * inverse)
        return ((lin_sum, real_sum, imag_sum), None)

    zeros = jnp.zeros((LAGS, pair_rows), jnp.float32)
    (lin_sum, real_sum, imag_sum), _ = lax.scan(one_day, (zeros, zeros, zeros), (gathered, weights))
    lin_all, real_all, imag_all, count_all = lax.psum(
        (lin_sum, real_sum, imag_sum, count_local), "day"
    )
    count_own = lax.dynamic_slice_in_dim(count_all, start, owned, 1)
    lin_own = lax.dynamic_slice_in_dim(lin_all, start, owned, 1)
    real_own = lax.dynamic_slice_in_dim(real_all, start, owned, 1)
    imag_own = lax.dynamic_slice_in_dim(imag_all, start, owned, 1)
    linear_stack = lin_own / count_own
    weighted_stack = (
        linear_stack * (real_own * real_own + imag_own * imag_own) / (count_own * count_own)
    )
    return (linear_stack, weighted_stack)


def solution(mesh):
    in_specs = (P("day", "pair", None), P("pair", None), P("day", None))
    out_specs = (P(None, ("pair", "day")), P(None, ("pair", "day")))
    return jax.shard_map(
        per_device, mesh=mesh, in_specs=in_specs, out_specs=out_specs, check_vma=False
    )
```

profile of v0, /device:TPU:1, one launch (start us, length us, event | category | flops | bytes accessed | tf_op | source)
XLA Modules:
  0.0 1000.1 jit_solution(7769191489236309300)
XLA Ops:
  8.0 3.7 negate_convert_fusion
  11.7 1.4 maximum_maximum_fusion
  13.7 92.6 %all-gather.2.cloned.1.call-done = bf16[4,128,1024]{2,1,0:T(8,128)(2,1)} async-done(((bf16[4,16,1024]{2,1,0:T(8,128)(2,1)}), bf16[4,128,1024]{2,1,0:T(8,128)(2,1)}) %all-gather.2.cloned.1.call-update) | async-done | bytes 1048592 | tf_op jit(solution)/shard_map/all_gather | solution.py:26
  106.3 48.9 %while.15 = (s32[]{:T(128)}, f32[401,512]{1,0:T(8,128)}, f32[401,512]{1,0:T(8,128)}, f32[401,512]{1,0:T(8,128)}, f32[4,512]{1,0:T(4,128)S(1)}, /*index=5*/bf16[4...) while((s32[]{:T(128)}, f32[401,512]{1,0:T(8,128)}, ...), condition=%wide.region_1.3_spmd.clone, body=%wide.region_0.2_spmd.clone.sunk | while | flops 850545664 | bytes 46903560 | solution.py:68
  107.3 2.1 gather_fusion
  109.6 2.1 gather_fusion.1
  114.8 1.8 select_add_fusion.4
  118.7 2.1 gather_fusion
  121.0 2.1 gather_fusion.1
  126.1 2.9 select_add_fusion.4
  131.2 2.1 gather_fusion
  133.5 2.1 gather_fusion.1
  137.2 1.0 convolution_bitcast_fusion.2
  138.6 2.9 select_add_fusion.4
  143.7 2.1 gather_fusion
  146.0 2.1 gather_fusion.1
  149.8 1.0 convolution_bitcast_fusion.2
  151.2 2.9 select_add_fusion.4
  155.3 2.6 copy.5
  157.9 1.3 copy.6
  159.2 1.4 copy.7
  160.6 212.1 %psum.29 = f32[1,512]{1,0:T(1,128)S(1)} all-reduce(f32[1,512]{1,0:T(1,128)S(1)} %bitcast.28), channel_id=1, replica_groups=mesh['day'=64,'pair'=8] {'day'}, use_global_device_ids=true, to_apply=%region_4.6 | all-reduce | flops 512 | bytes 4096 | tf_op jit(solution)/shard_map/psum | solution.py:69
  372.7 619.1 %all-reduce.3.cloned.1.call-done = (f32[401,512]{0,1:T(8,128)}, f32[401,512]{0,1:T(8,128)}, f32[401,512]{0,1:T(8,128)}) async-done(((f32[401,512]{0,1:T(8,128)}, f32[401,512]{0,1:T(8,128)}, f32[401,512]{0,1:T(8,128)}), (f32[401,512]{0,1:T(8,128)}, f32[401,512]{0,1:T(8,128)}, f32[401,512]{0,1:T(8,128)})) %all-reduce.3.cloned.1.call-update) | async-done | bytes 2463760 | tf_op jit(solution)/shard_map/psum | solution.py:69
  991.8 1.4 multiply_divide_fusion
  (98 shorter events, 20.8 us)
Async XLA Ops:
  7.2 99.2 %all-gather.2.cloned.1.call-start = ((), (), s32[]{:S(2)}) async-start(), calls=%async_computation | async-start | bytes 1179648 | tf_op jit(solution)/shard_map/all_gather | solution.py:26
  7.9 5.3 copy-start.7
  7.9 5.3 copy-start.8
  7.9 983.9 %all-reduce.3.cloned.1.call-start = ((), (), s32[]{:S(2)}) async-start(), calls=%async_computation.1 | async-start | bytes 6291456 | tf_op jit(solution)/shard_map/psum | solution.py:69
  111.9 1.4 copy-start.6
  113.4 1.1 copy-start
  113.4 1.4 copy-start.2
  116.5 0.9 copy-start.1
  116.5 1.2 copy-start.3
  123.3 1.4 copy-start.6
  124.7 1.1 copy-start
  124.7 1.4 copy-start.2
  129.0 0.9 copy-start.1
  129.0 1.2 copy-start.3
  135.8 1.4 copy-start.6
  137.2 1.1 copy-start
  137.2 1.4 copy-start.2
  141.6 1.2 copy-start.3
  148.3 1.4 copy-start.6
  149.8 1.1 copy-start
  149.8 1.4 copy-start.2
  154.1 1.2 copy-start.3
  155.3 2.6 copy-start.4
  155.3 3.9 copy-start.5
  (2 other events, 1.8 us)
Sparse Core Ops, SparseCore 0:
  11.2 95.0 all-gather.1
  160.7 831.0 all-reduce.2
where the time goes:
time: 1000 us
  waiting for transfers between devices  712 us (71%)
  blocking collectives  212 us (21%)
  local copies, waits for them, and re-layouts  35.1 us (4%)
  other arithmetic  21.2 us (2%)
  between operations  14.1 us (1%)
    psum x1, waiting for transfers between devices, per_device(): lax.psum((lin_sum, real_sum, imag_sum, count_local), 'day')  619 us
    psum x1, blocking collectives, per_device(): lax.psum((lin_sum, real_sum, imag_sum, count_local), 'day')  212 us
    all_gather x1, waiting for transfers between devices, per_device(): gathered = lax.all_gather(spectra, 'pair', axis=1, tiled=True)  92.6 us
  transfers between devices with their start and end apart: 2, of which 2 were waited for; matrix products, arithmetic and copies ran while one was open for 1% of the time, Pallas kernels for 0%

commit v1 on v0

--- a/solution.py
+++ b/solution.py
@@ -35,10 +35,7 @@
     weights = jnp.einsum("ds,ps->dp", mask_float, pick_first) * jnp.einsum(
         "ds,ps->dp", mask_float, pick_second
     )
-    count_local = jnp.sum(weights, 0, keepdims=True)
-    groups = lax.axis_size("day")
-    owned = pair_rows // groups
-    start = lax.axis_index("day") * owned
+    count_local = jnp.sum(weights, 0)[:, None]
     table = lag_table()
 
     def one_day(carry, inputs):
@@ -52,32 +49,32 @@
         cross_im = left_im * right_re - left_re * right_im
         cross = jnp.concatenate([cross_re, cross_im], 1).astype(jnp.bfloat16)
         analytic = lax.dot_general(
-            table, cross, (((1,), (1,)), ((), ())), preferred_element_type=jnp.float32
+            cross, table, (((1,), (1,)), ((), ())), preferred_element_type=jnp.float32
         )
-        trace = analytic[:LAGS]
-        hilbert = analytic[LAGS:]
+        trace = analytic[:, :LAGS]
+        hilbert = analytic[:, LAGS:]
         amplitude = jnp.sqrt(trace * trace + hilbert * hilbert)
         inverse = 1.0 / jnp.maximum(amplitude, 0.5)
+        w = weight[:, None]
         lin_sum, real_sum, imag_sum = carry
-        lin_sum = lin_sum + weight[None, :] * trace
-        real_sum = real_sum + weight[None, :] * (trace * inverse)
-        imag_sum = imag_sum + weight[None, :] * (hilbert * inverse)
+        lin_sum = lin_sum + w * trace
+        real_sum = real_sum + w * (trace * inverse)
+        imag_sum = imag_sum + w * (hilbert * inverse)
         return ((lin_sum, real_sum, imag_sum), None)
 
-    zeros = jnp.zeros((LAGS, pair_rows), jnp.float32)
+    zeros = jnp.zeros((pair_rows, LAGS), jnp.float32)
     (lin_sum, real_sum, imag_sum), _ = lax.scan(one_day, (zeros, zeros, zeros), (gathered, weights))
-    lin_all, real_all, imag_all, count_all = lax.psum(
-        (lin_sum, real_sum, imag_sum, count_local), "day"
-    )
-    count_own = lax.dynamic_slice_in_dim(count_all, start, owned, 1)
-    lin_own = lax.dynamic_slice_in_dim(lin_all, start, owned, 1)
-    real_own = lax.dynamic_slice_in_dim(real_all, start, owned, 1)
-    imag_own = lax.dynamic_slice_in_dim(imag_all, start, owned, 1)
+    packed = jnp.concatenate([lin_sum, real_sum, imag_sum, count_local], 1)
+    own = lax.psum_scatter(packed, "day", scatter_dimension=0, tiled=True)
+    lin_own = own[:, :LAGS]
+    real_own = own[:, LAGS : 2 * LAGS]
+    imag_own = own[:, 2 * LAGS : 3 * LAGS]
+    count_own = own[:, 3 * LAGS :]
     linear_stack = lin_own / count_own
     weighted_stack = (
         linear_stack * (real_own * real_own + imag_own * imag_own) / (count_own * count_own)
     )
-    return (linear_stack, weighted_stack)
+    return (linear_stack.T, weighted_stack.T)
 
 
 def solution(mesh):

time: 1000 us -> 605 us (0.60)
  blocking collectives: 212 us -> 0 us
  waiting for transfers between devices: 712 us -> 513 us
    psum x1 -> x0, waiting for transfers between devices: 619 us -> none  [per_device(): lax.psum((lin_sum, real_sum, imag_sum, count_local), 'day')]
    reduce_scatter x0 -> x1, waiting for transfers between devices: none -> 423 us  [per_device(): own = lax.psum_scatter(packed, 'day', scatter_dimension=0, tiled=True)]
    psum x1 -> x0, blocking collectives: 212 us -> none  [per_device(): lax.psum((lin_sum, real_sum, imag_sum, count_local), 'day')]
where the time goes in v1:
time: 605 us; the launch traced here: 595 us
  waiting for transfers between devices  513 us (85%)
  local copies, waits for them, and re-layouts  39.5 us (7%)
  other arithmetic  22.1 us (4%)
  between operations  14.1 us (2%)
  matrix products  6.06 us (1%)
    reduce_scatter x1, waiting for transfers between devices, per_device(): own = lax.psum_scatter(packed, 'day', scatter_dimension=0, tiled=True)  423 us
    all_gather x1, waiting for transfers between devices, per_device(): gathered = lax.all_gather(spectra, 'pair', axis=1, tiled=True)  89.7 us
  transfers between devices with their start and end apart: 2, of which 2 were waited for; matrix products, arithmetic and copies ran while one was open for 1% of the time, Pallas kernels for 0%

profile of v1, /device:TPU:1, one launch (start us, length us, event | category | flops | bytes accessed | tf_op | source)
XLA Modules:
  0.0 595.3 jit_solution(12339247741243256172)
XLA Ops:
  11.5 3.7 negate_convert_fusion
  15.2 1.4 maximum_maximum_fusion
  16.6 89.7 %all-gather.2.cloned.1.call-done = bf16[4,128,1024]{2,1,0:T(8,128)(2,1)} async-done(((bf16[4,16,1024]{2,1,0:T(8,128)(2,1)}), bf16[4,128,1024]{2,1,0:T(8,128)(2,1)}) %all-gather.2.cloned.1.call-update) | async-done | bytes 1048592 | tf_op jit(solution)/shard_map/all_gather | solution.py:26
  106.3 48.9 %while.15 = (s32[]{:T(128)}, f32[512,401]{0,1:T(8,128)}, f32[512,401]{0,1:T(8,128)}, f32[512,401]{0,1:T(8,128)}, f32[4,512]{1,0:T(4,128)S(1)}, /*index=5*/bf16[4...) while((s32[]{:T(128)}, f32[512,401]{0,1:T(8,128)}, ...), condition=%wide.region_1.3_spmd.clone, body=%wide.region_0.2_spmd.clone.sunk | while | flops 850545664 | bytes 46903560 | solution.py:66
  107.3 2.1 gather_fusion
  109.6 2.1 gather_fusion.1
  114.8 1.8 select_add_fusion.4
  118.7 2.1 gather_fusion
  121.0 2.1 gather_fusion.1
  124.7 1.0 fusion.30
  126.1 2.9 select_add_fusion.4
  131.2 2.1 gather_fusion
  133.5 2.1 gather_fusion.1
  138.6 2.9 select_add_fusion.4
  143.7 2.1 gather_fusion
  146.0 2.1 gather_fusion.1
  149.7 1.0 fusion.30
  151.1 2.9 select_add_fusion.4
  155.2 1.6 copy.10
  156.9 1.3 copy.8
  158.2 1.3 copy.9
  159.5 3.8 concatenate.22
  163.3 422.7 %reduce-scatter.2.cloned.1.call-done = f32[8,1204]{1,0:T(8,128)} async-done(((f32[512,1204]{1,0:T(8,128)}), f32[8,1204]{1,0:T(8,128)}) %reduce-scatter.2.cloned.1.call-update) | async-done | bytes 38544 | tf_op jit(solution)/shard_map/reduce_scatter | solution.py:68
  586.9 1.5 fusion.18
  (99 shorter events, 24.7 us)
Async XLA Ops:
  7.2 99.2 %all-gather.2.cloned.1.call-start = ((), (), s32[]{:S(2)}) async-start(), calls=%async_computation.1 | async-start | bytes 1179648 | tf_op jit(solution)/shard_map/all_gather | solution.py:26
  7.9 578.1 %reduce-scatter.2.cloned.1.call-start = ((), (), s32[]{:S(2)}) async-start(), calls=%async_computation.2 | async-start | bytes 2662400 | tf_op jit(solution)/shard_map/reduce_scatter | solution.py:68
  111.9 1.4 copy-start.7
  113.4 1.1 copy-start
  113.4 1.4 copy-start.3
  116.5 0.9 copy-start.1
  116.5 1.2 copy-start.4
  123.3 1.4 copy-start.7
  124.7 1.1 copy-start
  124.7 1.4 copy-start.3
  129.0 1.2 copy-start.4
  135.8 1.4 copy-start.7
  137.2 1.1 copy-start
  137.2 1.4 copy-start.3
  141.5 0.9 copy-start.1
  141.5 1.2 copy-start.4
  148.3 1.4 copy-start.7
  149.7 1.1 copy-start
  149.7 1.4 copy-start.3
  154.0 1.2 copy-start.4
  155.2 1.6 copy-start.2
  155.2 2.9 copy-start.5
  156.8 2.7 copy-start.8
  158.2 1.3 copy-start.6
  (2 other events, 1.8 us)
Sparse Core Ops, SparseCore 0:
  11.2 95.0 all-gather.1
  163.4 422.5 reduce-scatter.1

commit v2 on v1

--- a/solution.py
+++ b/solution.py
@@ -23,7 +23,8 @@
 
 
 def per_device(spectra, pair_list, mask):
-    gathered = lax.all_gather(spectra, "pair", axis=1, tiled=True)
+    g = lax.all_gather(spectra, "zh", axis=1, tiled=True)
+    gathered = lax.all_gather(g, "y", axis=1, tiled=True)
     station_count = gathered.shape[1]
     pair_rows = pair_list.shape[0]
     first = pair_list[:, 0]
@@ -65,7 +66,11 @@
     zeros = jnp.zeros((pair_rows, LAGS), jnp.float32)
     (lin_sum, real_sum, imag_sum), _ = lax.scan(one_day, (zeros, zeros, zeros), (gathered, weights))
     packed = jnp.concatenate([lin_sum, real_sum, imag_sum, count_local], 1)
-    own = lax.psum_scatter(packed, "day", scatter_dimension=0, tiled=True)
+    cols = packed.shape[1]
+    p = packed.reshape(4, 8, 2, 8, cols).transpose(2, 1, 0, 3, 4).reshape(512, cols)
+    p = lax.psum_scatter(p, "c", scatter_dimension=0, tiled=True)
+    p = lax.psum_scatter(p, "zl", scatter_dimension=0, tiled=True)
+    own = lax.psum_scatter(p, "x", scatter_dimension=0, tiled=True)
     lin_own = own[:, :LAGS]
     real_own = own[:, LAGS : 2 * LAGS]
     imag_own = own[:, 2 * LAGS : 3 * LAGS]
@@ -78,8 +83,11 @@
 
 
 def solution(mesh):
-    in_specs = (P("day", "pair", None), P("pair", None), P("day", None))
-    out_specs = (P(None, ("pair", "day")), P(None, ("pair", "day")))
-    return jax.shard_map(
-        per_device, mesh=mesh, in_specs=in_specs, out_specs=out_specs, check_vma=False
-    )
+    from jax.sharding import Mesh
+    devs = mesh.devices.reshape(4, 8, 2, 4, 2)
+    m = Mesh(devs, ("x", "zl", "c", "y", "zh"))
+    day = ("x", "zl", "c")
+    pair = ("y", "zh")
+    in_specs = (P(day, pair, None), P(pair, None), P(day, None))
+    out_specs = (P(None, pair + day), P(None, pair + day))
+    return jax.shard_map(per_device, mesh=m, in_specs=in_specs, out_specs=out_specs, check_vma=False)

time: 605 us -> 253 us (0.42); the launches traced: 595 us -> 251 us
  waiting for transfers between devices: 513 us -> 147 us
  blocking collectives: 0 us -> 20.1 us
    reduce_scatter x1 -> x3, waiting for transfers between devices: 423 us -> 117 us  [the longest x1 65.7 us: per_device(): p = lax.psum_scatter(p, 'zl', scatter_dimension=0, tiled=True)]
    all_gather x1, waiting for transfers between devices: 89.7 us -> 29.6 us  [per_device(): gathered = lax.all_gather(g, 'y', axis=1, tiled=True)]
    all_gather x0 -> x1, blocking collectives: none -> 20.1 us  [per_device(): g = lax.all_gather(spectra, 'zh', axis=1, tiled=True)]
  transfers between devices with their start and end apart: 2 -> 4, of which waited for: 2 -> 4; matrix products, arithmetic and copies ran while one was open for 1% -> 3% of each run, Pallas kernels for 0% -> 0%
where the time goes in v2:
time: 253 us; the launch traced here: 251 us
  waiting for transfers between devices  147 us (58%)
  local copies, waits for them, and re-layouts  41.6 us (16%)
  other arithmetic  22 us (9%)
  blocking collectives  20.1 us (8%)
  between operations  13.8 us (5%)
  matrix products  6.06 us (2%)
    reduce_scatter x1, waiting for transfers between devices, per_device(): p = lax.psum_scatter(p, 'zl', scatter_dimension=0, tiled=True)  65.7 us
    all_gather x1, waiting for transfers between devices, per_device(): gathered = lax.all_gather(g, 'y', axis=1, tiled=True)  29.6 us
    reduce_scatter x1, waiting for transfers between devices, per_device(): own = lax.psum_scatter(p, 'x', scatter_dimension=0, tiled=True)  28.4 us
    reduce_scatter x1, waiting for transfers between devices, per_device(): p = lax.psum_scatter(p, 'c', scatter_dimension=0, tiled=True)  23.2 us
    all_gather x1, blocking collectives, per_device(): g = lax.all_gather(spectra, 'zh', axis=1, tiled=True)  20.1 us
    add x4, other arithmetic, one_day(): imag_sum = imag_sum + w * (hilbert * inverse)  10.4 us
    while x40, local copies, waits for them, and re-layouts  9.36 us
    gather x4, local copies, waits for them, and re-layouts, one_day(): right = jnp.take(day_spec, second, axis=0).astype(jnp.float32)  8.23 us
  transfers between devices with their start and end apart: 4, of which 4 were waited for; matrix products, arithmetic and copies ran while one was open for 3% of the time, Pallas kernels for 0%

profile of v2, /device:TPU:1, one launch (start us, length us, event | category | flops | bytes accessed | tf_op | source)
XLA Modules:
  0.0 251.1 jit_solution(6080571666313189166)
XLA Ops:
  7.2 20.1 %all_gather.6 = bf16[4,32,1024]{2,1,0:T(8,128)(2,1)} all-gather(bf16[4,16,1024]{2,1,0:T(8,128)(2,1)} %param.7), channel_id=1, replica_groups=mesh['x'=4,'zl'=8,'c'=2,'y'=4,'zh'=2] {'zh'}, dimensions={1}, use_global_device_ids=true | all-gather | bytes 393216 | tf_op jit(solution)/shard_map/all_gather | solution.py:26
  31.0 3.7 %negate_convert_fusion = (bf16[401,512]{1,0:T(8,128)(2,1)S(1)}, bf16[401,512]{1,0:T(8,128)(2,1)S(1)}, bf16[401,512]{1,0:T(8,128)(2,1)S(1)}) fusion(s32[401]{0:T(512)S(1)} %iota_add_fusion), kind=kLoop, calls=%fused_computation.31 | loop fusion | flops 4106240 | bytes 1233476 | tf_op jit(solution)/shard_map/convert.7
  34.8 1.4 maximum_maximum_fusion
  36.2 29.6 %all-gather.2.cloned.1.call-done = bf16[4,128,1024]{2,1,0:T(8,128)(2,1)} async-done(((bf16[4,32,1024]{2,1,0:T(8,128)(2,1)}), bf16[4,128,1024]{2,1,0:T(8,128)(2,1)}) %all-gather.2.cloned.1.call-update) | async-done | bytes 1048592 | tf_op jit(solution)/shard_map/all_gather | solution.py:27
  65.8 48.8 %while.15 = (s32[]{:T(128)}, f32[512,401]{0,1:T(8,128)}, f32[512,401]{0,1:T(8,128)}, f32[512,401]{0,1:T(8,128)}, f32[4,512]{1,0:T(4,128)S(1)}, /*index=5*/bf16[4...) while((s32[]{:T(128)}, f32[512,401]{0,1:T(8,128)}, ...), condition=%wide.region_1.3_spmd.clone, body=%wide.region_0.2_spmd.clone.sunk | while | flops 850545664 | bytes 46903560 | solution.py:67
  66.8 2.1 gather_fusion
  69.1 2.1 gather_fusion.1
  74.2 1.7 select_add_fusion.4
  78.1 2.1 gather_fusion
  80.4 2.1 gather_fusion.1
  85.6 2.9 %select_add_fusion.4 = (f32[512,401]{0,1:T(8,128)}, f32[512,401]{0,1:T(8,128)S(1)}, f32[512,401]{0,1:T(8,128)S(1)}) fusion(f32[512,401]{0,1:T(8,128)} %get-tuple-element.210, f32[512,802]{0,1:T(8,128)S(1)} %fusion.30, f32[512]{0:T(512)S(1)} %bitcast.31, pred[]{:T(512)S(6)} %compare.4, f32[512,401]{0,1:T(8,128)S(1)} %copy-done.2, ...), kind=kLoop, calls=%fused_computation.10.clone.1 | loop fusion | flops 3284992 | bytes 6572033 | tf_op jit(solution)/shard_map/while/body/eval_jaxpr/add | solution.py:63
  90.6 2.1 gather_fusion
  92.9 2.1 gather_fusion.1
  98.1 2.9 %select_add_fusion.4 = (f32[512,401]{0,1:T(8,128)}, f32[512,401]{0,1:T(8,128)S(1)}, f32[512,401]{0,1:T(8,128)S(1)}) fusion(f32[512,401]{0,1:T(8,128)} %get-tuple-element.210, f32[512,802]{0,1:T(8,128)S(1)} %fusion.30, f32[512]{0:T(512)S(1)} %bitcast.31, pred[]{:T(512)S(6)} %compare.4, f32[512,401]{0,1:T(8,128)S(1)} %copy-done.2, ...), kind=kLoop, calls=%fused_computation.10.clone.1 | loop fusion | flops 3284992 | bytes 6572033 | tf_op jit(solution)/shard_map/while/body/eval_jaxpr/add | solution.py:63
  103.1 2.1 gather_fusion
  105.4 2.1 gather_fusion.1
  110.5 2.9 %select_add_fusion.4 = (f32[512,401]{0,1:T(8,128)}, f32[512,401]{0,1:T(8,128)S(1)}, f32[512,401]{0,1:T(8,128)S(1)}) fusion(f32[512,401]{0,1:T(8,128)} %get-tuple-element.210, f32[512,802]{0,1:T(8,128)S(1)} %fusion.30, f32[512]{0:T(512)S(1)} %bitcast.31, pred[]{:T(512)S(6)} %compare.4, f32[512,401]{0,1:T(8,128)S(1)} %copy-done.2, ...), kind=kLoop, calls=%fused_computation.10.clone.1 | loop fusion | flops 3284992 | bytes 6572033 | tf_op jit(solution)/shard_map/while/body/eval_jaxpr/add | solution.py:63
  114.6 2.6 %copy.12 = f32[512,401]{1,0:T(8,128)} copy(f32[512,401]{0,1:T(8,128)} %get-tuple-element.52) | data formatting | bytes 1642496 | tf_op jit(solution)/shard_map/while | solution.py:67
  119.8 3.1 %concatenate.35 = f32[4,8,2,8,1204]{4,3,2,1,0:T(8,128)S(1)} concatenate(f32[4,8,2,8,401]{4,3,2,1,0:T(8,128)} %bitcast.24, f32[4,8,2,8,401]{4,3,2,1,0:T(8,128)} %bitcast.25, f32[4,8,2,8,401]{4,3,2,1,0:T(8,128)} %bitcast.26, f32[4,8,2,8,1]{4,3,2,1,0:T(8,128)S(1)} %copy-done.7), dimensions={4} | concatenate | bytes 4931584 | tf_op jit(solution)/shard_map/concatenate | solution.py:68
  123.0 1.8 copy.16
  124.8 23.2 %reduce-scatter.4.cloned.1.call-done = f32[256,1204]{1,0:T(8,128)} async-done(((f32[512,1204]{1,0:T(8,128)}), f32[256,1204]{1,0:T(8,128)}) %reduce-scatter.4.cloned.1.call-update) | async-done | bytes 1232912 | tf_op jit(solution)/shard_map/reduce_scatter | solution.py:71
  148.1 65.7 %reduce-scatter.6.cloned.1.call-done = f32[32,1204]{1,0:T(8,128)} async-done(((f32[256,1204]{1,0:T(8,128)}), f32[32,1204]{1,0:T(8,128)}) %reduce-scatter.6.cloned.1.call-update) | async-done | bytes 154128 | tf_op jit(solution)/shard_map/reduce_scatter | solution.py:72
  213.8 28.4 %reduce-scatter.8.cloned.1.call-done = f32[8,1204]{1,0:T(8,128)} async-done(((f32[32,1204]{1,0:T(8,128)}), f32[8,1204]{1,0:T(8,128)}) %reduce-scatter.8.cloned.1.call-update) | async-done | bytes 38544 | tf_op jit(solution)/shard_map/reduce_scatter | solution.py:73
  243.1 1.5 fusion.18
  (105 shorter events, 28.9 us)
Async XLA Ops:
  7.2 58.6 %all-gather.2.cloned.1.call-start = ((), (), s32[]{:S(2)}) async-start(), calls=%async_computation.3 | async-start | bytes 1310720 | tf_op jit(solution)/shard_map/all_gather | solution.py:27
  27.4 120.7 %reduce-scatter.4.cloned.1.call-start = ((), (), s32[]{:S(2)}) async-start(), calls=%async_computation.4 | async-start | bytes 3932160 | tf_op jit(solution)/shard_map/reduce_scatter | solution.py:71
  71.4 1.4 copy-start.6
  72.8 1.1 copy-start
  72.8 1.4 copy-start.2
  76.0 0.9 copy-start.1
  76.0 1.2 copy-start.3
  82.7 1.4 copy-start.6
  84.2 1.1 copy-start
  84.2 1.4 copy-start.2
  88.5 1.2 copy-start.3
  95.2 1.4 copy-start.6
  96.6 1.1 copy-start
  96.7 1.4 copy-start.2
  100.9 1.2 copy-start.3
  107.7 1.4 copy-start.6
  109.1 1.1 copy-start
  109.1 1.4 copy-start.2
  113.4 1.2 copy-start.3
  114.6 2.6 %copy-start.4 = (f32[512,401]{0,1:T(8,128)S(1)}, f32[512,401]{0,1:T(8,128)}, u32[]{:S(2)}) copy-start(f32[512,401]{0,1:T(8,128)} %get-tuple-element.53) | copy-start | bytes 2463748
  114.6 3.9 %copy-start.5 = (f32[512,401]{0,1:T(8,128)S(1)}, f32[512,401]{0,1:T(8,128)}, u32[]{:S(2)}) copy-start(f32[512,401]{0,1:T(8,128)} %get-tuple-element.54) | copy-start | bytes 2463748
  117.2 2.7 %copy-start.7 = (f32[4,8,2,8,1]{4,3,2,1,0:T(8,128)S(1)}, f32[4,8,2,8,1]{4,3,2,1,0:T(8,128)}, u32[]{:S(2)}) copy-start(f32[4,8,2,8,1]{4,3,2,1,0:T(8,128)} %concatenate.37) | copy-start | bytes 6148
  124.8 89.0 %reduce-scatter.6.cloned.1.call-start = ((), (), s32[]{:S(2)}) async-start(), calls=%async_computation.5 | async-start | bytes 1474560 | tf_op jit(solution)/shard_map/reduce_scatter | solution.py:72
  148.1 94.1 %reduce-scatter.8.cloned.1.call-start = ((), (), s32[]{:S(2)}) async-start(), calls=%async_computation.6 | async-start | bytes 204800 | tf_op jit(solution)/shard_map/reduce_scatter | solution.py:73
  (3 other events, 2.7 us)
Sparse Core Ops, SparseCore 0:
  27.5 38.2 all-gather.1
  124.9 23.1 reduce-scatter.3
  151.2 62.5 reduce-scatter.5
  216.7 25.4 reduce-scatter.7

commit v3 on v2

--- a/solution.py
+++ b/solution.py
@@ -24,11 +24,19 @@
 
 def per_device(spectra, pair_list, mask):
     g = lax.all_gather(spectra, "zh", axis=1, tiled=True)
-    gathered = lax.all_gather(g, "y", axis=1, tiled=True)
+    g = lax.all_gather(g, "y", axis=1, tiled=True)
+    gathered = lax.all_gather(g, "c", axis=0, tiled=True)
+    mask = lax.all_gather(mask, "c", axis=0, tiled=True)
+    core = lax.axis_index("c")
+    nx, nz, nc = 4, 8, 2
+    k = pair_list.shape[0] // (nx * nz * nc)
+    pl = pair_list.reshape(nx, nz, nc, k, 2)
+    pl = lax.dynamic_index_in_dim(pl, core, 2, keepdims=False)
+    pl = pl.transpose(1, 0, 2, 3).reshape(nz * nx * k, 2)
     station_count = gathered.shape[1]
-    pair_rows = pair_list.shape[0]
-    first = pair_list[:, 0]
-    second = pair_list[:, 1]
+    pair_rows = pl.shape[0]
+    first = pl[:, 0]
+    second = pl[:, 1]
     column = lax.broadcasted_iota(jnp.int32, (pair_rows, station_count), 1)
     pick_first = (first[:, None] == column).astype(jnp.float32)
     pick_second = (second[:, None] == column).astype(jnp.float32)
@@ -67,10 +75,7 @@
     (lin_sum, real_sum, imag_sum), _ = lax.scan(one_day, (zeros, zeros, zeros), (gathered, weights))
     packed = jnp.concatenate([lin_sum, real_sum, imag_sum, count_local], 1)
     cols = packed.shape[1]
-    p = packed.reshape(4, 8, 2, 8, cols).transpose(2, 1, 0, 3, 4).reshape(512, cols)
-    p = lax.psum_scatter(p, "c", scatter_dimension=0, tiled=True)
-    p = lax.psum_scatter(p, "zl", scatter_dimension=0, tiled=True)
-    own = lax.psum_scatter(p, "x", scatter_dimension=0, tiled=True)
+    own = lax.all_to_all(packed.reshape(32, -1, cols), ("zl", "x"), 0, 0, tiled=True).sum(0)
     lin_own = own[:, :LAGS]
     real_own = own[:, LAGS : 2 * LAGS]
     imag_own = own[:, 2 * LAGS : 3 * LAGS]

time: 253 us -> 228 us (0.901)
  waiting for transfers between devices: 147 us -> 55 us
  blocking collectives: 20.1 us -> 97.5 us
  other arithmetic: 22 us -> 14.2 us
    reduce_scatter x3 -> x0, waiting for transfers between devices: 117 us -> none  [the longest x1 65.7 us: per_device(): p = lax.psum_scatter(p, 'zl', scatter_dimension=0, tiled=True)]
    all_to_all x0 -> x1, blocking collectives: none -> 74.3 us  [per_device(): lax.all_to_all(packed.reshape(32, -1, cols), ('zl', 'x'), 0, 0, tiled=True)]
    all_gather x1 -> x2, waiting for transfers between devices: 29.6 us -> 55 us  [the longest x1 38.4 us: per_device(): g = lax.all_gather(g, 'y', axis=1, tiled=True)]
    add x4 -> x8, other arithmetic: 10.4 us -> 3.56 us  [one_day(): imag_sum = imag_sum + w * (hilbert * inverse)]
    squeeze x4 -> x8, local copies, waits for them, and re-layouts: 3.87 us -> 7.77 us  [per_device(): lax.scan(one_day, (zeros, zeros, zeros), (gathered, weights))]
    while x3, local copies, waits for them, and re-layouts: 5.23 us -> 1.38 us  [per_device(): lax.scan(one_day, (zeros, zeros, zeros), (gathered, weights))]
    all_gather x0 -> x1, blocking collectives: none -> 3.06 us  [per_device(): mask = lax.all_gather(mask, 'c', axis=0, tiled=True)]
    gather x4 -> x8, local copies, waits for them, and re-layouts: 8.23 us -> 9.35 us  [one_day(): right = jnp.take(day_spec, second, axis=0).astype(jnp.float32)]
  transfers between devices with their start and end apart: 4 -> 2, of which waited for: 4 -> 2; matrix products, arithmetic and copies ran while one was open for 3% -> 3% of each run, Pallas kernels for 0% -> 0%
where the time goes in v3:
time: 228 us; the launch traced here: 227 us
  blocking collectives  97.5 us (43%)
  waiting for transfers between devices  55 us (24%)
  local copies, waits for them, and re-layouts  39.2 us (17%)
  other arithmetic  14.2 us (6%)
  between operations  14.2 us (6%)
  matrix products  5.51 us (2%)
    all_to_all x1, blocking collectives, per_device(): lax.all_to_all(packed.reshape(32, -1, cols), ('zl', 'x'), 0, 0, tiled=True)  74.3 us
    all_gather x1, waiting for transfers between devices, per_device(): g = lax.all_gather(g, 'y', axis=1, tiled=True)  38.4 us
    all_gather x1, blocking collectives, per_device(): g = lax.all_gather(spectra, 'zh', axis=1, tiled=True)  20.1 us
    all_gather x1, waiting for transfers between devices, per_device(): gathered = lax.all_gather(g, 'c', axis=0, tiled=True)  16.6 us
    gather x8, local copies, waits for them, and re-layouts, one_day(): right = jnp.take(day_spec, second, axis=0).astype(jnp.float32)  9.35 us
    gather x8, local copies, waits for them, and re-layouts, one_day(): left = jnp.take(day_spec, first, axis=0).astype(jnp.float32)  9.35 us
    while x16, local copies, waits for them, and re-layouts  9.25 us
    squeeze x8, local copies, waits for them, and re-layouts, per_device(): lax.scan(one_day, (zeros, zeros, zeros), (gathered, weights))  7.77 us
  transfers between devices with their start and end apart: 2, of which 2 were waited for; matrix products, arithmetic and copies ran while one was open for 3% of the time, Pallas kernels for 0%

profile of v3, /device:TPU:1, one launch (start us, length us, event | category | flops | bytes accessed | tf_op | source)
XLA Modules:
  0.0 226.6 jit_solution(8053150763884239593)
XLA Ops:
  7.2 20.1 %all_gather.13 = bf16[4,32,1024]{2,1,0:T(8,128)(2,1)} all-gather(bf16[4,16,1024]{2,1,0:T(8,128)(2,1)} %param.7), channel_id=1, replica_groups=mesh['x'=4,'zl'=8,'c'=2,'y'=4,'zh'=2] {'zh'}, dimensions={1}, use_global_device_ids=true | all-gather | bytes 393216 | tf_op jit(solution)/shard_map/all_gather | solution.py:26
  27.4 38.4 %all-gather.4.cloned.1.call-done = bf16[4,128,1024]{2,1,0:T(8,128)(2,1)} async-done(((bf16[4,32,1024]{2,1,0:T(8,128)(2,1)}), bf16[4,128,1024]{2,1,0:T(8,128)(2,1)}) %all-gather.4.cloned.1.call-update) | async-done | bytes 1048592 | tf_op jit(solution)/shard_map/all_gather | solution.py:27
  66.2 3.1 %all-gather = s32[2,4,128]{2,1,0:T(4,128)S(1)} all-gather(s32[1,4,128]{2,1,0:T(4,128)S(1)} %bitcast.43), channel_id=1, replica_groups=mesh['x'=4,'zl'=8,'c'=2,'y'=4,'zh'=2] {'c'}, dimensions={0}, use_global_device_ids=true | all-gather | bytes 6144 | tf_op jit(solution)/shard_map/all_gather | solution.py:29
  70.0 3.7 %negate_convert_fusion = (bf16[401,512]{1,0:T(8,128)(2,1)S(1)}, bf16[401,512]{1,0:T(8,128)(2,1)S(1)}, bf16[401,512]{1,0:T(8,128)(2,1)S(1)}) fusion(s32[401]{0:T(512)S(1)} %iota_add_fusion), kind=kLoop, calls=%fused_computation.31 | loop fusion | flops 4106240 | bytes 1233476 | tf_op jit(solution)/shard_map/convert.7
  73.7 1.4 maximum_maximum_fusion
  75.1 16.6 %all-gather.6.cloned.1.call-done = bf16[8,128,1024]{2,1,0:T(8,128)(2,1)} async-done(((bf16[4,128,1024]{2,1,0:T(8,128)(2,1)}), bf16[8,128,1024]{2,1,0:T(8,128)(2,1)}) %all-gather.6.cloned.1.call-update) | async-done | bytes 2097168 | tf_op jit(solution)/shard_map/all_gather | solution.py:28
  91.7 49.8 %while.15 = (s32[]{:T(128)}, f32[256,401]{0,1:T(8,128)S(1)}, f32[256,401]{0,1:T(8,128)S(1)}, f32[256,401]{0,1:T(8,128)S(1)}, f32[8,256]{1,0:T(8,128)S(1)}, /*ind...) while((s32[]{:T(128)}, f32[256,401]{0,1:T(8,128)S(1)}, ...), condition=%wide.region_1.3_spmd.clone, body=%wide.region_0.0_spmd.clone.sunk | while | flops 425273856 | bytes 21254296 | solution.py:75
  92.7 1.2 gather_fusion
  94.1 1.2 gather_fusion.1
  98.9 1.2 gather_fusion
  100.3 1.2 gather_fusion.1
  105.2 1.2 gather_fusion
  106.5 1.2 gather_fusion.1
  111.4 1.2 gather_fusion
  112.8 1.2 gather_fusion.1
  117.6 1.2 gather_fusion
  119.0 1.2 gather_fusion.1
  123.9 1.2 gather_fusion
  125.2 1.2 gather_fusion.1
  130.1 1.2 gather_fusion
  131.4 1.2 gather_fusion.1
  136.3 1.2 gather_fusion
  143.0 1.5 concatenate.35
  144.5 74.3 %all_to_all.5 = f32[32,8,1204]{2,1,0:T(8,128)S(1)} all-to-all(f32[32,8,1204]{2,1,0:T(8,128)S(1)} %concatenate.35), channel_id=1, replica_groups=mesh['x'=4,'zl'=8,'c'=2,'y'=4,'zh'=2] {'zl','x'}, dimensions={0} | all-to-all | bytes 2465792 | tf_op jit(solution)/shard_map/all_to_all | solution.py:78
  (132 shorter events, 34.9 us)
Async XLA Ops:
  7.2 58.7 %copy-start.1 = (s32[512,2]{0,1:T(2,128)S(1)}, s32[512,2]{0,1:T(2,128)}, u32[]{:S(2)}) copy-start(s32[512,2]{0,1:T(2,128)} %param.8) | copy-start | bytes 12292
  7.2 59.0 %copy-start.2 = (s32[4,128]{1,0:T(4,128)S(1)}, s32[4,128]{1,0:T(4,128)}, u32[]{:S(2)}) copy-start(s32[4,128]{1,0:T(4,128)} %param.9) | copy-start | bytes 6148
  7.2 58.6 %all-gather.4.cloned.1.call-start = ((), (), s32[]{:S(2)}) async-start(), calls=%async_computation.1 | async-start | bytes 1310720 | tf_op jit(solution)/shard_map/all_gather | solution.py:27
  27.4 64.3 %all-gather.6.cloned.1.call-start = ((), (), s32[]{:S(2)}) async-start(), calls=%async_computation.2 | async-start | bytes 3145728 | tf_op jit(solution)/shard_map/all_gather | solution.py:28
  95.4 1.4 copy-start
  101.6 1.4 copy-start
  107.8 1.4 copy-start
  114.1 1.4 copy-start
  120.3 1.4 copy-start
  126.5 1.4 copy-start
  132.8 1.4 copy-start
  139.0 1.4 copy-start
Sparse Core Ops, SparseCore 0:
  27.5 38.2 all-gather.3
  67.9 23.7 all-gather.5

commit v4 on v3

v4 whole, which is shorter than its diff:
```python
import math

import jax
import jax.numpy as jnp
from jax import lax
from jax.sharding import PartitionSpec as P

F = 512
MAXLAG = 200
LAGS = 401


def lag_table():
    lag = jnp.arange(LAGS, dtype=jnp.int32) - MAXLAG
    freq = jnp.arange(F, dtype=jnp.int32)
    phase = jnp.mod(lag[:, None] * freq[None, :], 2 * F).astype(jnp.float32) * (math.pi / F)
    scale = 1.0 / math.sqrt(F)
    cosine = jnp.cos(phase) * scale
    sine = jnp.sin(phase) * scale
    upper = jnp.concatenate([cosine, -sine], 1)
    lower = jnp.concatenate([sine, cosine], 1)
    return jnp.concatenate([upper, lower], 0).astype(jnp.bfloat16)


def day_sums(days, mask_days, first, second, table):
    station_count = days.shape[1]
    pair_rows = first.shape[0]
    column = lax.broadcasted_iota(jnp.int32, (pair_rows, station_count), 1)
    pick_first = (first[:, None] == column).astype(jnp.float32)
    pick_second = (second[:, None] == column).astype(jnp.float32)
    mask_float = mask_days.astype(jnp.float32)
    weights = jnp.einsum("ds,ps->dp", mask_float, pick_first) * jnp.einsum(
        "ds,ps->dp", mask_float, pick_second
    )
    count = jnp.sum(weights, 0)[:, None]
    left = jnp.take(days, first, axis=1).astype(jnp.float32)
    right = jnp.take(days, second, axis=1).astype(jnp.float32)
    half = left.shape[2] // 2
    left_re, left_im = (left[..., :half], left[..., half:])
    right_re, right_im = (right[..., :half], right[..., half:])
    cross_re = left_re * right_re + left_im * right_im
    cross_im = left_im * right_re - left_re * right_im
    cross = jnp.concatenate([cross_re, cross_im], 2).astype(jnp.bfloat16)
    analytic = lax.dot_general(
        cross, table, (((2,), (1,)), ((), ())), preferred_element_type=jnp.float32
    )
    trace = analytic[..., :LAGS]
    hilbert = analytic[..., LAGS:]
    amplitude = jnp.sqrt(trace * trace + hilbert * hilbert)
    inverse = 1.0 / jnp.maximum(amplitude, 0.5)
    w = weights[:, :, None]
    lin_sum = jnp.sum(w * trace, 0)
    real_sum = jnp.sum(w * (trace * inverse), 0)
    imag_sum = jnp.sum(w * (hilbert * inverse), 0)
    return lin_sum, real_sum, imag_sum, count


def per_device(spectra, pair_list, mask):
    g = lax.all_gather(spectra, "zh", axis=1, tiled=True)
    g = lax.all_gather(g, "y", axis=1, tiled=True)
    core = lax.axis_index("c")
    swap = [(0, 1), (1, 0)]
    g_other = lax.ppermute(g, "c", swap)
    mask_other = lax.ppermute(mask, "c", swap)
    nx, nz, nc = 4, 8, 2
    k = pair_list.shape[0] // (nx * nz * nc)
    pl = pair_list.reshape(nx, nz, nc, k, 2)
    pl = lax.dynamic_index_in_dim(pl, core, 2, keepdims=False)
    pl = pl.transpose(1, 0, 2, 3).reshape(nz * nx * k, 2)
    first = pl[:, 0]
    second = pl[:, 1]
    table = lag_table()
    mine = day_sums(g, mask, first, second, table)
    theirs = day_sums(g_other, mask_other, first, second, table)
    sums = [a + b for a, b in zip(mine, theirs)]
    packed = jnp.concatenate(list(sums), 1)
    cols = packed.shape[1]
    own = lax.all_to_all(packed.reshape(32, -1, cols), ("zl", "x"), 0, 0, tiled=True).sum(0)
    lin_own = own[:, :LAGS]
    real_own = own[:, LAGS : 2 * LAGS]
    imag_own = own[:, 2 * LAGS : 3 * LAGS]
    count_own = own[:, 3 * LAGS :]
    linear_stack = lin_own / count_own
    weighted_stack = (
        linear_stack * (real_own * real_own + imag_own * imag_own) / (count_own * count_own)
    )
    return (linear_stack.T, weighted_stack.T)


def solution(mesh):
    from jax.sharding import Mesh
    devs = mesh.devices.reshape(4, 8, 2, 4, 2)
    m = Mesh(devs, ("x", "zl", "c", "y", "zh"))
    day = ("x", "zl", "c")
    pair = ("y", "zh")
    in_specs = (P(day, pair, None), P(pair, None), P(day, None))
    out_specs = (P(None, pair + day), P(None, pair + day))
    return jax.shard_map(per_device, mesh=m, in_specs=in_specs, out_specs=out_specs, check_vma=False)
```

time: 228 us -> 198 us (0.87)
  waiting for transfers between devices: 55 us -> 33.3 us
  local copies, waits for them, and re-layouts: 39.2 us -> 17.9 us
  starting transfers between devices: 0.08 us -> 9.42 us
  other arithmetic: 14.2 us -> 22.8 us
  blocking collectives: 97.5 us -> 93.6 us
    all_gather x1 -> x0, waiting for transfers between devices: 16.6 us -> none  [per_device(): gathered = lax.all_gather(g, 'c', axis=0, tiled=True)]
    while x19 -> x0, local copies, waits for them, and re-layouts: 10.6 us -> none
    convert_element_type x17 -> x2, other arithmetic: 2.22 us -> 12.1 us  [the longest x1 7.52 us: day_sums(): left = jnp.take(days, first, axis=1).astype(jnp.float32)]
    ppermute x0 -> x2, starting transfers between devices: none -> 9.38 us  [the longest x1 5.78 us: per_device(): mask_other = lax.ppermute(mask, 'c', swap)]
    squeeze x8 -> x0, local copies, waits for them, and re-layouts: 7.77 us -> none  [per_device(): lax.scan(one_day, (zeros, zeros, zeros), (gathered, weights))]
    all_gather x1, waiting for transfers between devices: 38.4 us -> 33.3 us  [per_device(): g = lax.all_gather(g, 'y', axis=1, tiled=True)]
    gather x16 -> x4, local copies, waits for them, and re-layouts: 18.7 us -> 14.4 us  [the longest x2 7.19 us: day_sums(): right = jnp.take(days, second, axis=1).astype(jnp.float32)]
    add x8 -> x4, other arithmetic: 3.56 us -> 0.17 us  [per_device(): sums = [a + b for a, b in zip(mine, theirs)]]
  transfers between devices with their start and end apart: 2 -> 3, of which waited for: 2 -> 1; matrix products, arithmetic and copies ran while one was open for 3% -> 8% of each run, Pallas kernels for 0% -> 0%
where the time goes in v4:
time: 198 us; the launch traced here: 197 us
  blocking collectives  93.6 us (47%)
  waiting for transfers between devices  33.3 us (17%)
  other arithmetic  22.8 us (12%)
  local copies, waits for them, and re-layouts  17.9 us (9%)
  between operations  14.3 us (7%)
  starting transfers between devices  9.42 us (5%)
  matrix products  6.12 us (3%)
    all_to_all x1, blocking collectives, per_device(): lax.all_to_all(packed.reshape(32, -1, cols), ('zl', 'x'), 0, 0, tiled=True)  75.8 us
    all_gather x1, waiting for transfers between devices, per_device(): g = lax.all_gather(g, 'y', axis=1, tiled=True)  33.3 us
    all_gather x1, blocking collectives, per_device(): g = lax.all_gather(spectra, 'zh', axis=1, tiled=True)  17.8 us
    convert_element_type x1, other arithmetic, day_sums(): left = jnp.take(days, first, axis=1).astype(jnp.float32)  7.52 us
    gather x2, local copies, waits for them, and re-layouts, day_sums(): right = jnp.take(days, second, axis=1).astype(jnp.float32)  7.19 us
    gather x2, local copies, waits for them, and re-layouts, day_sums(): left = jnp.take(days, first, axis=1).astype(jnp.float32)  7.16 us
    another operation x2, other arithmetic  7.09 us
    ppermute x1, starting transfers between devices, per_device(): mask_other = lax.ppermute(mask, 'c', swap)  5.78 us
  transfers between devices with their start and end apart: 3, of which 1 were waited for; matrix products, arithmetic and copies ran while one was open for 8% of the time, Pallas kernels for 0%

profile of v4, /device:TPU:1, one launch (start us, length us, event | category | flops | bytes accessed | tf_op | source)
XLA Modules:
  0.0 197.5 jit_solution(9146521412614867805)
XLA Ops:
  7.2 1.0 copy.19
  8.2 17.8 %all_gather.6 = bf16[4,32,1024]{2,0,1:T(4,128)(2,1)} all-gather(bf16[4,16,1024]{2,0,1:T(4,128)(2,1)S(1)} %copy.19), channel_id=1, replica_groups=mesh['x'=4,'zl'=8,'c'=2,'y'=4,'zh'=2] {'zh'}, dimensions={1}, use_global_device_ids=true | all-gather | bytes 393216 | tf_op jit(solution)/shard_map/all_gather | solution.py:59
  26.0 5.8 %collective-permute-start = (s32[4,128]{1,0:T(4,128)}, s32[4,128]{1,0:T(4,128)S(1)}, u32[]{:S(2)}, u32[]{:S(2)}) collective-permute-start(s32[4,128]{1,0:T(4,128)} %param.7), channel_id=1, source_target_pairs={{0,8},{8,0},{1,9},{9,1},{2,10},{10,2},{3,11},{11,3},{4,12},{12,4},... | collective-permute-start | bytes 6152 | tf_op jit(solution)/shard_map/ppermute | solution.py:64
  31.8 0.8 reshape.56
  32.9 0.9 fusion.16
  33.8 33.3 %all-gather.2.cloned.1.call-done = bf16[4,128,1024]{2,0,1:T(4,128)(2,1)} async-done(((bf16[4,32,1024]{2,0,1:T(4,128)(2,1)}), bf16[4,128,1024]{2,0,1:T(4,128)(2,1)}) %all-gather.2.cloned.1.call-update) | async-done | bytes 1048592 | tf_op jit(solution)/shard_map/all_gather | solution.py:60
  67.1 3.6 %collective-permute-start.1 = (bf16[4,128,1024]{2,0,1:T(4,128)(2,1)}, bf16[4,128,1024]{2,0,1:T(4,128)(2,1)S(1)}, u32[]{:S(2)}, u32[]{:S(2)}) collective-permute-start(bf16[4,128,1024]{2,0,1:T(4,128)(2,1)} %all-gather.2.cloned.1.call-done), channel_id=1, source_target_pairs={{0,8},{8,0},{1,9},{9,1},{2,10},{10,2},{3,11},{11,3},{4,12},{12,4},... | collective-permute-start | bytes 3145736 | tf_op jit(solution)/shard_map/ppermute | solution.py:63
  70.7 0.9 fusion.33
  71.6 4.6 %negate_convert_fusion = (bf16[401,512]{1,0:T(8,128)(2,1)}, bf16[401,512]{1,0:T(8,128)(2,1)}, bf16[401,512]{1,0:T(8,128)(2,1)}) fusion(s32[401]{0:T(512)S(1)} %iota_add_fusion), kind=kLoop, calls=%fused_computation.41 | loop fusion | flops 4106240 | bytes 1233476 | tf_op jit(solution)/shard_map/convert.7
  76.5 0.2 fusion.34
  76.9 3.6 %gather_fusion = bf16[256,4,1024]{2,1,0:T(4,128)(2,1)} fusion(bf16[4,128,1024]{2,0,1:T(4,128)(2,1)S(1)} %copy-done.2, s32[1024]{0:T(1024)S(1)} %pad_clamp_fusion.1), kind=kCustom, calls=%fused_computation.clone | custom fusion | bytes 4195328 | tf_op jit(solution)/shard_map/jit(_take)/gather | solution.py:36
  80.5 3.6 %gather_fusion.1 = bf16[256,4,1024]{2,1,0:T(4,128)(2,1)} fusion(bf16[4,128,1024]{2,0,1:T(4,128)(2,1)S(1)} %copy-done.2, s32[1024]{0:T(1024)S(1)} %pad_clamp_fusion), kind=kCustom, calls=%fused_computation.1.clone | custom fusion | bytes 4195328 | tf_op jit(solution)/shard_map/jit(_take)/gather | solution.py:37
  84.2 3.6 %gather_fusion.2 = bf16[256,4,1024]{2,1,0:T(4,128)(2,1)} fusion(bf16[4,128,1024]{2,0,1:T(4,128)(2,1)S(1)} %collective-permute-done.1, s32[1024]{0:T(1024)S(1)} %pad_clamp_fusion.1), kind=kCustom, calls=%fused_computation.2.clone | custom fusion | bytes 4195328 | tf_op jit(solution)/shard_map/jit(_take)/gather | solution.py:36
  87.7 7.5 %bitcast_convert_fusion.1 = (f32[4,256,1024]{2,1,0:T(8,128)}, f32[4,256,1024]{2,1,0:T(8,128)}) fusion(bf16[256,4,1024]{2,1,0:T(4,128)(2,1)} %gather_fusion.2, pred[256]{0:T(512)(128)(4,1)S(1)} %compare_and_fusion.1, bf16[256,4,1024]{2,1,0:T(4,128)(2,1)S(1)} %copy-done.4), kind=kLoop, calls=%fused_computation.13 | loop fusion | flops 4194304 | bytes 12583168 | tf_op jit(solution)/shard_map/convert_element_type | solution.py:36
  95.3 3.5 %gather_fusion.3 = bf16[256,4,1024]{2,1,0:T(4,128)(2,1)} fusion(bf16[4,128,1024]{2,0,1:T(4,128)(2,1)S(1)} %collective-permute-done.1, s32[1024]{0:T(1024)S(1)} %pad_clamp_fusion), kind=kCustom, calls=%fused_computation.3.clone | custom fusion | bytes 4195328 | tf_op jit(solution)/shard_map/jit(_take)/gather | solution.py:37
  98.8 4.6 %bitcast_convert_fusion = (f32[4,256,1024]{2,1,0:T(8,128)S(1)}, f32[4,256,1024]{2,1,0:T(8,128)S(1)}) fusion(bf16[256,4,1024]{2,1,0:T(4,128)(2,1)} %gather_fusion.3, pred[256]{0:T(512)(128)(4,1)S(1)} %compare_and_fusion, bf16[256,4,1024]{2,1,0:T(4,128)(2,1)S(1)} %copy-done.3), kind=kLoop, calls=%fused_computation.12 | loop fusion | flops 4194304 | bytes 12583168 | tf_op jit(solution)/shard_map/convert_element_type | solution.py:37
  103.5 2.5 %add_convert_fusion = (bf16[4,256,512]{2,1,0:T(8,128)(2,1)S(1)}, bf16[4,256,512]{2,1,0:T(8,128)(2,1)S(1)}, bf16[4,256,512]{2,1,0:T(8,128)(2,1)S(1)}, bf16[4,256,512]{2,1,0:T(8,128)(2,1)S(1)}) fusion(f32[4,256,1024]{2,1,0:T(8,128)S(1)} %get-tuple-element.24, f32[4,256,1024]{2,1,0:T(8,128)S(1)} %copy-done, f32[4,256,1024]{2,1,0:T(8,128)S(1)} %get-tuple-element.25, ...), kind=kLoop, calls=%fused_computation.21 | loop fusion | flops 8388608 | bytes 20971520 | tf_op jit(solution)/shard_map/convert
  106.0 1.9 fusion.4
  108.0 1.2 multiply_reduce_fusion
  109.2 1.9 fusion
  111.1 1.2 multiply_reduce_fusion.1
  113.1 0.7 concatenate.29
  113.8 75.8 %all_to_all.5 = f32[32,8,1204]{2,1,0:T(8,128)S(1)} all-to-all(f32[32,8,1204]{2,1,0:T(8,128)S(1)} %concatenate.29), channel_id=1, replica_groups=mesh['x'=4,'zl'=8,'c'=2,'y'=4,'zh'=2] {'zl','x'}, dimensions={0} | all-to-all | bytes 2465792 | tf_op jit(solution)/shard_map/all_to_all | solution.py:78
  189.9 0.7 fusion.24
  (42 shorter events, 1.7 us)
Async XLA Ops:
  7.2 59.9 %all-gather.2.cloned.1.call-start = ((), (), s32[]{:S(2)}) async-start(), calls=%async_computation.1 | async-start | bytes 1310720 | tf_op jit(solution)/shard_map/all_gather | solution.py:60
  26.0 50.2 %collective-permute-start = (s32[4,128]{1,0:T(4,128)}, s32[4,128]{1,0:T(4,128)S(1)}, u32[]{:S(2)}, u32[]{:S(2)}) collective-permute-start(s32[4,128]{1,0:T(4,128)} %param.7), channel_id=1, source_target_pairs={{0,8},{8,0},{1,9},{9,1},{2,10},{10,2},{3,11},{11,3},{4,12},{12,4},... | collective-permute-start | bytes 6152 | tf_op jit(solution)/shard_map/ppermute | solution.py:64
  67.1 9.8 %copy-start.2 = (bf16[4,128,1024]{2,0,1:T(4,128)(2,1)S(1)}, bf16[4,128,1024]{2,0,1:T(4,128)(2,1)}, u32[]{:S(2)}) copy-start(bf16[4,128,1024]{2,0,1:T(4,128)(2,1)} %all-gather.2.cloned.1.call-done) | copy-start | bytes 3145732
  67.1 17.1 %collective-permute-start.1 = (bf16[4,128,1024]{2,0,1:T(4,128)(2,1)}, bf16[4,128,1024]{2,0,1:T(4,128)(2,1)S(1)}, u32[]{:S(2)}, u32[]{:S(2)}) collective-permute-start(bf16[4,128,1024]{2,0,1:T(4,128)(2,1)} %all-gather.2.cloned.1.call-done), channel_id=1, source_target_pairs={{0,8},{8,0},{1,9},{9,1},{2,10},{10,2},{3,11},{11,3},{4,12},{12,4},... | collective-permute-start | bytes 3145736 | tf_op jit(solution)/shard_map/ppermute | solution.py:63
  84.2 3.6 %copy-start.4 = (bf16[256,4,1024]{2,1,0:T(4,128)(2,1)S(1)}, bf16[256,4,1024]{2,1,0:T(4,128)(2,1)}, u32[]{:S(2)}) copy-start(bf16[256,4,1024]{2,1,0:T(4,128)(2,1)} %gather_fusion) | copy-start | bytes 6291460
  95.3 3.6 %copy-start.3 = (bf16[256,4,1024]{2,1,0:T(4,128)(2,1)S(1)}, bf16[256,4,1024]{2,1,0:T(4,128)(2,1)}, u32[]{:S(2)}) copy-start(bf16[256,4,1024]{2,1,0:T(4,128)(2,1)} %gather_fusion.1) | copy-start | bytes 6291460
  98.8 4.6 %copy-start = (f32[4,256,1024]{2,1,0:T(8,128)S(1)}, f32[4,256,1024]{2,1,0:T(8,128)}, u32[]{:S(2)}) copy-start(f32[4,256,1024]{2,1,0:T(8,128)} %get-tuple-element.22) | copy-start | bytes 12582916
  98.8 4.6 %copy-start.1 = (f32[4,256,1024]{2,1,0:T(8,128)S(1)}, f32[4,256,1024]{2,1,0:T(8,128)}, u32[]{:S(2)}) copy-start(f32[4,256,1024]{2,1,0:T(8,128)} %get-tuple-element.23) | copy-start | bytes 12582916
  103.5 2.5 %copy-start.5 = (bf16[401,512]{1,0:T(8,128)(2,1)S(1)}, bf16[401,512]{1,0:T(8,128)(2,1)}, u32[]{:S(2)}) copy-start(bf16[401,512]{1,0:T(8,128)(2,1)} %get-tuple-element.17) | copy-start | bytes 1231876
  103.5 2.5 %copy-start.6 = (bf16[401,512]{1,0:T(8,128)(2,1)S(1)}, bf16[401,512]{1,0:T(8,128)(2,1)}, u32[]{:S(2)}) copy-start(bf16[401,512]{1,0:T(8,128)(2,1)} %get-tuple-element.18) | copy-start | bytes 1231876
  103.5 2.5 %copy-start.7 = (bf16[401,512]{1,0:T(8,128)(2,1)S(1)}, bf16[401,512]{1,0:T(8,128)(2,1)}, u32[]{:S(2)}) copy-start(bf16[401,512]{1,0:T(8,128)(2,1)} %get-tuple-element.19) | copy-start | bytes 1231876
Sparse Core Ops, SparseCore 0:
  26.1 40.9 all-gather.1

commit v5 on v4

--- a/solution.py
+++ b/solution.py
@@ -75,7 +75,8 @@
     sums = [a + b for a, b in zip(mine, theirs)]
     packed = jnp.concatenate(list(sums), 1)
     cols = packed.shape[1]
-    own = lax.all_to_all(packed.reshape(32, -1, cols), ("zl", "x"), 0, 0, tiled=True).sum(0)
+    p = lax.all_to_all(packed.reshape(8, 4, -1, cols).transpose(1, 0, 2, 3), "x", 0, 0, tiled=True).sum(0)
+    own = lax.all_to_all(p, "zl", 0, 0, tiled=True).sum(0)
     lin_own = own[:, :LAGS]
     real_own = own[:, LAGS : 2 * LAGS]
     imag_own = own[:, 2 * LAGS : 3 * LAGS]

time: 198 us -> 172 us (0.87)
  blocking collectives: 93.6 us -> 66 us
    all_to_all x1 -> x2, blocking collectives: 75.8 us -> 48.2 us  [the longest x1 26.7 us: per_device(): own = lax.all_to_all(p, 'zl', 0, 0, tiled=True).sum(0)]
  transfers between devices with their start and end apart: 3 -> 3, of which waited for: 1 -> 1; matrix products, arithmetic and copies ran while one was open for 8% -> 9% of each run, Pallas kernels for 0% -> 0%
where the time goes in v5:
time: 172 us; the launch traced here: 170 us
  blocking collectives  66 us (38%)
  waiting for transfers between devices  33.3 us (19%)
  other arithmetic  22.9 us (13%)
  local copies, waits for them, and re-layouts  18 us (10%)
  between operations  14.3 us (8%)
  starting transfers between devices  9.42 us (5%)
  matrix products  6.12 us (4%)
    all_gather x1, waiting for transfers between devices, per_device(): g = lax.all_gather(g, 'y', axis=1, tiled=True)  33.3 us
    all_to_all x1, blocking collectives, per_device(): own = lax.all_to_all(p, 'zl', 0, 0, tiled=True).sum(0)  26.7 us
    all_to_all x1, blocking collectives, per_device(): lax.all_to_all(packed.reshape(8, 4, -1, cols).transpose(1, 0, 2, 3), 'x',...  21.5 us
    all_gather x1, blocking collectives, per_device(): g = lax.all_gather(spectra, 'zh', axis=1, tiled=True)  17.8 us
    convert_element_type x1, other arithmetic, day_sums(): left = jnp.take(days, first, axis=1).astype(jnp.float32)  7.52 us
    gather x2, local copies, waits for them, and re-layouts, day_sums(): right = jnp.take(days, second, axis=1).astype(jnp.float32)  7.2 us
    gather x2, local copies, waits for them, and re-layouts, day_sums(): left = jnp.take(days, first, axis=1).astype(jnp.float32)  7.16 us
    another operation x2, other arithmetic  7.09 us
  transfers between devices with their start and end apart: 3, of which 1 were waited for; matrix products, arithmetic and copies ran while one was open for 9% of the time, Pallas kernels for 0%

profile of v5, /device:TPU:1, one launch (start us, length us, event | category | flops | bytes accessed | tf_op | source)
XLA Modules:
  0.0 170.0 jit_solution(13490573211436306255)
XLA Ops:
  7.2 1.0 copy.34
  8.2 17.8 %all_gather.6 = bf16[4,32,1024]{2,0,1:T(4,128)(2,1)} all-gather(bf16[4,16,1024]{2,0,1:T(4,128)(2,1)S(1)} %copy.34), channel_id=1, replica_groups=mesh['x'=4,'zl'=8,'c'=2,'y'=4,'zh'=2] {'zh'}, dimensions={1}, use_global_device_ids=true | all-gather | bytes 393216 | tf_op jit(solution)/shard_map/all_gather | solution.py:59
  26.0 5.8 %collective-permute-start = (s32[4,128]{1,0:T(4,128)}, s32[4,128]{1,0:T(4,128)S(1)}, u32[]{:S(2)}, u32[]{:S(2)}) collective-permute-start(s32[4,128]{1,0:T(4,128)} %param.7), channel_id=1, source_target_pairs={{0,8},{8,0},{1,9},{9,1},{2,10},{10,2},{3,11},{11,3},{4,12},{12,4},... | collective-permute-start | bytes 6152 | tf_op jit(solution)/shard_map/ppermute | solution.py:64
  31.8 0.8 reshape.56
  32.9 0.9 fusion.16
  33.8 33.3 %all-gather.2.cloned.1.call-done = bf16[4,128,1024]{2,0,1:T(4,128)(2,1)} async-done(((bf16[4,32,1024]{2,0,1:T(4,128)(2,1)}), bf16[4,128,1024]{2,0,1:T(4,128)(2,1)}) %all-gather.2.cloned.1.call-update) | async-done | bytes 1048592 | tf_op jit(solution)/shard_map/all_gather | solution.py:60
  67.1 3.6 %collective-permute-start.1 = (bf16[4,128,1024]{2,0,1:T(4,128)(2,1)}, bf16[4,128,1024]{2,0,1:T(4,128)(2,1)S(1)}, u32[]{:S(2)}, u32[]{:S(2)}) collective-permute-start(bf16[4,128,1024]{2,0,1:T(4,128)(2,1)} %all-gather.2.cloned.1.call-done), channel_id=1, source_target_pairs={{0,8},{8,0},{1,9},{9,1},{2,10},{10,2},{3,11},{11,3},{4,12},{12,4},... | collective-permute-start | bytes 3145736 | tf_op jit(solution)/shard_map/ppermute | solution.py:63
  70.7 0.9 fusion.33
  71.6 4.6 %negate_convert_fusion = (bf16[401,512]{1,0:T(8,128)(2,1)}, bf16[401,512]{1,0:T(8,128)(2,1)}, bf16[401,512]{1,0:T(8,128)(2,1)}) fusion(s32[401]{0:T(512)S(1)} %iota_add_fusion), kind=kLoop, calls=%fused_computation.41 | loop fusion | flops 4106240 | bytes 1233476 | tf_op jit(solution)/shard_map/convert.7
  76.9 3.6 %gather_fusion = bf16[256,4,1024]{2,1,0:T(4,128)(2,1)} fusion(bf16[4,128,1024]{2,0,1:T(4,128)(2,1)S(1)} %copy-done.2, s32[1024]{0:T(1024)S(1)} %pad_clamp_fusion.1), kind=kCustom, calls=%fused_computation.clone | custom fusion | bytes 4195328 | tf_op jit(solution)/shard_map/jit(_take)/gather | solution.py:36
  80.5 3.6 %gather_fusion.1 = bf16[256,4,1024]{2,1,0:T(4,128)(2,1)} fusion(bf16[4,128,1024]{2,0,1:T(4,128)(2,1)S(1)} %copy-done.2, s32[1024]{0:T(1024)S(1)} %pad_clamp_fusion), kind=kCustom, calls=%fused_computation.1.clone | custom fusion | bytes 4195328 | tf_op jit(solution)/shard_map/jit(_take)/gather | solution.py:37
  84.2 3.5 %gather_fusion.2 = bf16[256,4,1024]{2,1,0:T(4,128)(2,1)} fusion(bf16[4,128,1024]{2,0,1:T(4,128)(2,1)S(1)} %collective-permute-done.1, s32[1024]{0:T(1024)S(1)} %pad_clamp_fusion.1), kind=kCustom, calls=%fused_computation.2.clone | custom fusion | bytes 4195328 | tf_op jit(solution)/shard_map/jit(_take)/gather | solution.py:36
  87.7 7.5 %bitcast_convert_fusion.1 = (f32[4,256,1024]{2,1,0:T(8,128)}, f32[4,256,1024]{2,1,0:T(8,128)}) fusion(bf16[256,4,1024]{2,1,0:T(4,128)(2,1)} %gather_fusion.2, pred[256]{0:T(512)(128)(4,1)S(1)} %compare_and_fusion.1, bf16[256,4,1024]{2,1,0:T(4,128)(2,1)S(1)} %copy-done.4), kind=kLoop, calls=%fused_computation.13 | loop fusion | flops 4194304 | bytes 12583168 | tf_op jit(solution)/shard_map/convert_element_type | solution.py:36
  95.3 3.5 %gather_fusion.3 = bf16[256,4,1024]{2,1,0:T(4,128)(2,1)} fusion(bf16[4,128,1024]{2,0,1:T(4,128)(2,1)S(1)} %collective-permute-done.1, s32[1024]{0:T(1024)S(1)} %pad_clamp_fusion), kind=kCustom, calls=%fused_computation.3.clone | custom fusion | bytes 4195328 | tf_op jit(solution)/shard_map/jit(_take)/gather | solution.py:37
  98.8 4.6 %bitcast_convert_fusion = (f32[4,256,1024]{2,1,0:T(8,128)S(1)}, f32[4,256,1024]{2,1,0:T(8,128)S(1)}) fusion(bf16[256,4,1024]{2,1,0:T(4,128)(2,1)} %gather_fusion.3, pred[256]{0:T(512)(128)(4,1)S(1)} %compare_and_fusion, bf16[256,4,1024]{2,1,0:T(4,128)(2,1)S(1)} %copy-done.3), kind=kLoop, calls=%fused_computation.12 | loop fusion | flops 4194304 | bytes 12583168 | tf_op jit(solution)/shard_map/convert_element_type | solution.py:37
  103.5 2.5 %add_convert_fusion = (bf16[4,256,512]{2,1,0:T(8,128)(2,1)S(1)}, bf16[4,256,512]{2,1,0:T(8,128)(2,1)S(1)}, bf16[4,256,512]{2,1,0:T(8,128)(2,1)S(1)}, bf16[4,256,512]{2,1,0:T(8,128)(2,1)S(1)}) fusion(f32[4,256,1024]{2,1,0:T(8,128)S(1)} %get-tuple-element.24, f32[4,256,1024]{2,1,0:T(8,128)S(1)} %copy-done, f32[4,256,1024]{2,1,0:T(8,128)S(1)} %get-tuple-element.25, ...), kind=kLoop, calls=%fused_computation.21 | loop fusion | flops 8388608 | bytes 20971520 | tf_op jit(solution)/shard_map/convert
  106.0 1.9 %fusion.4 = f32[4,256,802]{1,2,0:T(8,128)S(1)} fusion(bf16[4,256,512]{2,1,0:T(8,128)(2,1)S(1)} %get-tuple-element.12, bf16[4,256,512]{2,1,0:T(8,128)(2,1)S(1)} %get-tuple-element.11, bf16[401,512]{1,0:T(8,128)(2,1)S(1)} %copy-done.7, bf16[401,512]{1,0:T(8,128)(2,1)S(1)} %copy-done.6, bf16[401,512]{1,0:T(8,128)(2,1)S(1)} %copy-done.5), kind=kOutput, calls=%fused_computation.8 | convolution fusion | flops 1692680192 | bytes 6614016 | tf_op jit(solution)/shard_map/dot_general | solution.py:44
  108.0 1.2 multiply_reduce_fusion
  109.2 1.9 %fusion = f32[4,256,802]{1,2,0:T(8,128)S(1)} fusion(bf16[4,256,512]{2,1,0:T(8,128)(2,1)S(1)} %get-tuple-element.30, bf16[4,256,512]{2,1,0:T(8,128)(2,1)S(1)} %get-tuple-element.31, bf16[401,512]{1,0:T(8,128)(2,1)S(1)} %copy-done.7, bf16[401,512]{1,0:T(8,128)(2,1)S(1)} %copy-done.6, bf16[401,512]{1,0:T(8,128)(2,1)S(1)} %copy-done.5), kind=kOutput, calls=%fused_computation.4 | convolution fusion | flops 1692680192 | bytes 6614016 | tf_op jit(solution)/shard_map/dot_general | solution.py:44
  111.1 1.2 multiply_reduce_fusion.1
  113.1 0.7 concatenate.29
  114.0 21.5 %all_to_all.10 = f32[4,8,8,1204]{3,2,1,0:T(8,128)S(1)} all-to-all(f32[4,8,8,1204]{3,2,1,0:T(8,128)S(1)} %copy.43), channel_id=1, replica_groups=mesh['x'=4,'zl'=8,'c'=2,'y'=4,'zh'=2] {'x'}, dimensions={0} | all-to-all | bytes 2465792 | tf_op jit(solution)/shard_map/all_to_all | solution.py:78
  135.6 26.7 %all_to_all.11 = f32[8,8,1204]{2,1,0:T(8,128)S(1)} all-to-all(f32[8,8,1204]{2,1,0:T(8,128)S(1)} %reduce_sum.98), channel_id=1, replica_groups=mesh['x'=4,'zl'=8,'c'=2,'y'=4,'zh'=2] {'zl'}, dimensions={0} | all-to-all | bytes 616448 | tf_op jit(solution)/shard_map/all_to_all | solution.py:79
  162.5 0.7 fusion.24
  (45 shorter events, 2.1 us)
Async XLA Ops:
  7.2 59.9 %all-gather.2.cloned.1.call-start = ((), (), s32[]{:S(2)}) async-start(), calls=%async_computation.2 | async-start | bytes 1310720 | tf_op jit(solution)/shard_map/all_gather | solution.py:60
  26.0 50.2 %collective-permute-start = (s32[4,128]{1,0:T(4,128)}, s32[4,128]{1,0:T(4,128)S(1)}, u32[]{:S(2)}, u32[]{:S(2)}) collective-permute-start(s32[4,128]{1,0:T(4,128)} %param.7), channel_id=1, source_target_pairs={{0,8},{8,0},{1,9},{9,1},{2,10},{10,2},{3,11},{11,3},{4,12},{12,4},... | collective-permute-start | bytes 6152 | tf_op jit(solution)/shard_map/ppermute | solution.py:64
  67.1 9.8 %copy-start.2 = (bf16[4,128,1024]{2,0,1:T(4,128)(2,1)S(1)}, bf16[4,128,1024]{2,0,1:T(4,128)(2,1)}, u32[]{:S(2)}) copy-start(bf16[4,128,1024]{2,0,1:T(4,128)(2,1)} %all-gather.2.cloned.1.call-done) | copy-start | bytes 3145732
  67.1 17.1 %collective-permute-start.1 = (bf16[4,128,1024]{2,0,1:T(4,128)(2,1)}, bf16[4,128,1024]{2,0,1:T(4,128)(2,1)S(1)}, u32[]{:S(2)}, u32[]{:S(2)}) collective-permute-start(bf16[4,128,1024]{2,0,1:T(4,128)(2,1)} %all-gather.2.cloned.1.call-done), channel_id=1, source_target_pairs={{0,8},{8,0},{1,9},{9,1},{2,10},{10,2},{3,11},{11,3},{4,12},{12,4},... | collective-permute-start | bytes 3145736 | tf_op jit(solution)/shard_map/ppermute | solution.py:63
  84.2 3.6 %copy-start.4 = (bf16[256,4,1024]{2,1,0:T(4,128)(2,1)S(1)}, bf16[256,4,1024]{2,1,0:T(4,128)(2,1)}, u32[]{:S(2)}) copy-start(bf16[256,4,1024]{2,1,0:T(4,128)(2,1)} %gather_fusion) | copy-start | bytes 6291460
  95.3 3.6 %copy-start.3 = (bf16[256,4,1024]{2,1,0:T(4,128)(2,1)S(1)}, bf16[256,4,1024]{2,1,0:T(4,128)(2,1)}, u32[]{:S(2)}) copy-start(bf16[256,4,1024]{2,1,0:T(4,128)(2,1)} %gather_fusion.1) | copy-start | bytes 6291460
  98.8 4.6 %copy-start = (f32[4,256,1024]{2,1,0:T(8,128)S(1)}, f32[4,256,1024]{2,1,0:T(8,128)}, u32[]{:S(2)}) copy-start(f32[4,256,1024]{2,1,0:T(8,128)} %get-tuple-element.22) | copy-start | bytes 12582916
  98.8 4.6 %copy-start.1 = (f32[4,256,1024]{2,1,0:T(8,128)S(1)}, f32[4,256,1024]{2,1,0:T(8,128)}, u32[]{:S(2)}) copy-start(f32[4,256,1024]{2,1,0:T(8,128)} %get-tuple-element.23) | copy-start | bytes 12582916
  103.5 2.5 %copy-start.5 = (bf16[401,512]{1,0:T(8,128)(2,1)S(1)}, bf16[401,512]{1,0:T(8,128)(2,1)}, u32[]{:S(2)}) copy-start(bf16[401,512]{1,0:T(8,128)(2,1)} %get-tuple-element.17) | copy-start | bytes 1231876
  103.5 2.5 %copy-start.6 = (bf16[401,512]{1,0:T(8,128)(2,1)S(1)}, bf16[401,512]{1,0:T(8,128)(2,1)}, u32[]{:S(2)}) copy-start(bf16[401,512]{1,0:T(8,128)(2,1)} %get-tuple-element.18) | copy-start | bytes 1231876
  103.5 2.5 %copy-start.7 = (bf16[401,512]{1,0:T(8,128)(2,1)S(1)}, bf16[401,512]{1,0:T(8,128)(2,1)}, u32[]{:S(2)}) copy-start(bf16[401,512]{1,0:T(8,128)(2,1)} %get-tuple-element.19) | copy-start | bytes 1231876
Sparse Core Ops, SparseCore 0:
  26.1 40.9 all-gather.1

commit v6 on v5

--- a/solution.py
+++ b/solution.py
@@ -33,8 +33,12 @@
         "ds,ps->dp", mask_float, pick_second
     )
     count = jnp.sum(weights, 0)[:, None]
-    left = jnp.take(days, first, axis=1).astype(jnp.float32)
-    right = jnp.take(days, second, axis=1).astype(jnp.float32)
+    left = jnp.einsum(
+        "ps,dsf->dpf", pick_first.astype(days.dtype), days, preferred_element_type=jnp.float32
+    )
+    right = jnp.einsum(
+        "ps,dsf->dpf", pick_second.astype(days.dtype), days, preferred_element_type=jnp.float32
+    )
     half = left.shape[2] // 2
     left_re, left_im = (left[..., :half], left[..., half:])
     right_re, right_im = (right[..., :half], right[..., half:])

time: 172 us -> 142 us (0.83)
  local copies, waits for them, and re-layouts: 18 us -> 2.6 us
  other arithmetic: 22.9 us -> 10.1 us
  waiting for transfers between devices: 33.3 us -> 28.3 us
  matrix products: 6.12 us -> 9.6 us
  blocking collectives: 66 us -> 68.3 us
  starting transfers between devices: 9.42 us -> 7.35 us
    gather x4 -> x0, local copies, waits for them, and re-layouts: 14.4 us -> none  [the longest x2 7.2 us: day_sums(): right = jnp.take(days, second, axis=1).astype(jnp.float32)]
    convert_element_type x2 -> x0, other arithmetic: 12.1 us -> none  [the longest x1 7.52 us: day_sums(): left = jnp.take(days, first, axis=1).astype(jnp.float32)]
    all_gather x1, waiting for transfers between devices: 33.3 us -> 28.3 us  [per_device(): g = lax.all_gather(g, 'y', axis=1, tiled=True)]
    dot_general x0 -> x4, matrix products: none -> 4.19 us  [the longest x2 2.7 us: day_sums(): jnp.einsum('ps,dsf->dpf', pick_second.astype(days.dtype), days, preferred...]
    all_gather x1, blocking collectives: 17.8 us -> 20.1 us  [per_device(): g = lax.all_gather(spectra, 'zh', axis=1, tiled=True)]
    ppermute x1, starting transfers between devices: 5.78 us -> 3.53 us  [per_device(): mask_other = lax.ppermute(mask, 'c', swap)]
    another operation x2 -> x3, other arithmetic: 7.09 us -> 6.18 us
where the time goes in v6:
time: 142 us; the launch traced here: 141 us
  blocking collectives  68.3 us (48%)
  waiting for transfers between devices  28.3 us (20%)
  between operations  14.3 us (10%)
  other arithmetic  10.1 us (7%)
  matrix products  9.6 us (7%)
  starting transfers between devices  7.35 us (5%)
  local copies, waits for them, and re-layouts  2.6 us (2%)
    all_gather x1, waiting for transfers between devices, per_device(): g = lax.all_gather(g, 'y', axis=1, tiled=True)  28.3 us
    all_to_all x1, blocking collectives, per_device(): own = lax.all_to_all(p, 'zl', 0, 0, tiled=True).sum(0)  26.7 us
    all_to_all x1, blocking collectives, per_device(): lax.all_to_all(packed.reshape(8, 4, -1, cols).transpose(1, 0, 2, 3), 'x',...  21.5 us
    all_gather x1, blocking collectives, per_device(): g = lax.all_gather(spectra, 'zh', axis=1, tiled=True)  20.1 us
    another operation x3, other arithmetic  6.18 us
    dot_general x2, matrix products, day_sums(): lax.dot_general(cross, table, (((2,), (1,)), ((), ())), preferred_element...  3.82 us
    ppermute x1, starting transfers between devices, per_device(): g_other = lax.ppermute(g, 'c', swap)  3.79 us
    ppermute x1, starting transfers between devices, per_device(): mask_other = lax.ppermute(mask, 'c', swap)  3.53 us
  transfers between devices with their start and end apart: 3, of which 1 were waited for; matrix products, arithmetic and copies ran while one was open for 9% of the time, Pallas kernels for 0%

profile of v6, /device:TPU:1, one launch (start us, length us, event | category | flops | bytes accessed | tf_op | source)
XLA Modules:
  0.0 140.6 jit_solution(12291015583892407385)
XLA Ops:
  7.2 20.1 %all_gather.6 = bf16[4,32,1024]{2,1,0:T(8,128)(2,1)} all-gather(bf16[4,16,1024]{2,1,0:T(8,128)(2,1)} %param.3), channel_id=1, replica_groups=mesh['x'=4,'zl'=8,'c'=2,'y'=4,'zh'=2] {'zh'}, dimensions={1}, use_global_device_ids=true | all-gather | bytes 393216 | tf_op jit(solution)/shard_map/all_gather | solution.py:63
  27.4 3.5 %collective-permute-start = (s32[4,128]{1,0:T(4,128)}, s32[4,128]{1,0:T(4,128)S(1)}, u32[]{:S(2)}, u32[]{:S(2)}) collective-permute-start(s32[4,128]{1,0:T(4,128)} %param.5), channel_id=1, source_target_pairs={{0,8},{8,0},{1,9},{9,1},{2,10},{10,2},{3,11},{11,3},{4,12},{12,4},... | collective-permute-start | bytes 6152 | tf_op jit(solution)/shard_map/ppermute | solution.py:68
  30.9 0.8 reshape.51
  32.0 0.9 fusion.16
  32.9 3.7 %negate_convert_fusion = (bf16[401,512]{1,0:T(8,128)(2,1)S(1)}, bf16[401,512]{1,0:T(8,128)(2,1)S(1)}, bf16[401,512]{1,0:T(8,128)(2,1)S(1)}) fusion(s32[401]{0:T(512)S(1)} %iota_add_fusion), kind=kLoop, calls=%fused_computation.33 | loop fusion | flops 4106240 | bytes 1233476 | tf_op jit(solution)/shard_map/convert.7
  36.6 0.2 fusion.43
  36.8 0.2 fusion.15
  37.0 0.2 fusion.44
  37.3 0.2 add.87
  37.5 28.3 %all-gather.2.cloned.1.call-done = bf16[4,128,1024]{2,1,0:T(8,128)(2,1)} async-done(((bf16[4,32,1024]{2,1,0:T(8,128)(2,1)}), bf16[4,128,1024]{2,1,0:T(8,128)(2,1)}) %all-gather.2.cloned.1.call-update) | async-done | bytes 1048592 | tf_op jit(solution)/shard_map/all_gather | solution.py:64
  65.8 3.8 %collective-permute-start.1 = (bf16[4,128,1024]{2,1,0:T(8,128)(2,1)}, bf16[4,128,1024]{2,1,0:T(8,128)(2,1)S(1)}, u32[]{:S(2)}, u32[]{:S(2)}) collective-permute-start(bf16[4,128,1024]{2,1,0:T(8,128)(2,1)} %all-gather.2.cloned.1.call-done), channel_id=1, source_target_pairs={{0,8},{8,0},{1,9},{9,1},{2,10},{10,2},{3,11},{11,3},{4,12},{12,4},... | collective-permute-start | bytes 3145736 | tf_op jit(solution)/shard_map/ppermute | solution.py:67
  69.6 2.0 %convolution_bitcast_fusion.2 = f32[4,256,1024]{2,1,0:T(8,128)S(1)} fusion(bf16[4,128,1024]{2,1,0:T(8,128)(2,1)} %all-gather.2.cloned.1.call-done, s32[256]{0:T(256)S(1)} %bitcast.52), kind=kOutput, calls=%fused_computation.2 | convolution fusion | flops 268533760 | bytes 5243904 | tf_op jit(solution)/shard_map/ps,dsf->dpf/dot_general | solution.py:39
  71.6 0.7 convolution_bitcast_fusion.3
  72.3 1.2 add_convert_fusion.1
  73.6 1.9 %fusion = f32[4,256,802]{1,2,0:T(8,128)S(1)} fusion(bf16[4,256,512]{2,1,0:T(8,128)(2,1)S(1)} %get-tuple-element.13, bf16[4,256,512]{2,1,0:T(8,128)(2,1)S(1)} %get-tuple-element.12, bf16[401,512]{1,0:T(8,128)(2,1)S(1)} %get-tuple-element.18, bf16[401,512]{1,0:T(8,128)(2,1)S(1)} %get-tuple-element.17, bf16[401,512]{1,0:T(8,128)(2,1)S(1)} %get-tuple-element.16), kind=kOutput, calls=%fused_computation.4 | convolution fusion | flops 1692680192 | bytes 6614016 | tf_op jit(solution)/shard_map/dot_general | solution.py:48
  75.5 0.7 convolution_bitcast_fusion.1
  76.2 0.7 convolution_bitcast_fusion
  77.0 1.2 add_convert_fusion
  78.2 1.9 %fusion.4 = f32[4,256,802]{1,2,0:T(8,128)S(1)} fusion(bf16[4,256,512]{2,1,0:T(8,128)(2,1)S(1)} %get-tuple-element.11, bf16[4,256,512]{2,1,0:T(8,128)(2,1)S(1)} %get-tuple-element.10, bf16[401,512]{1,0:T(8,128)(2,1)S(1)} %get-tuple-element.18, bf16[401,512]{1,0:T(8,128)(2,1)S(1)} %get-tuple-element.17, bf16[401,512]{1,0:T(8,128)(2,1)S(1)} %get-tuple-element.16), kind=kOutput, calls=%fused_computation.8 | convolution fusion | flops 1692680192 | bytes 6614016 | tf_op jit(solution)/shard_map/dot_general | solution.py:48
  80.1 2.8 %multiply_reduce_fusion = (f32[256,401]{0,1:T(8,128)S(1)}, f32[256,401]{0,1:T(8,128)S(1)}, f32[256,401]{0,1:T(8,128)S(1)}, f32[256,401]{0,1:T(8,128)S(1)}, f32[256,401]{0,1:T(8,128)S(1)}, /*index=5*/f32[256,401]{0,1:T(8,128)S(1)}) fusion(f32[4,256,802]{1,2,0:T(8,128)S(1)} %fusion.4, f32[4,256]{1,0:T(4,128)S(1)} %bitcast.59, f32[4,256,802]{1,2,0:T(8,128)S(1)} %fusion, ...), kind=kLoop, calls=%fused_computation.16 | loop fusion | flops 10060288 | bytes 9041920 | tf_op jit(solution)/shard_map/reduce_sum | solution.py:58
  83.7 0.7 concatenate.29
  84.6 21.5 %all_to_all.10 = f32[4,8,8,1204]{3,2,1,0:T(8,128)S(1)} all-to-all(f32[4,8,8,1204]{3,2,1,0:T(8,128)S(1)} %copy.23), channel_id=1, replica_groups=mesh['x'=4,'zl'=8,'c'=2,'y'=4,'zh'=2] {'x'}, dimensions={0} | all-to-all | bytes 2465792 | tf_op jit(solution)/shard_map/all_to_all | solution.py:82
  106.2 26.7 %all_to_all.11 = f32[8,8,1204]{2,1,0:T(8,128)S(1)} all-to-all(f32[8,8,1204]{2,1,0:T(8,128)S(1)} %reduce_sum.98), channel_id=1, replica_groups=mesh['x'=4,'zl'=8,'c'=2,'y'=4,'zh'=2] {'zl'}, dimensions={0} | all-to-all | bytes 616448 | tf_op jit(solution)/shard_map/all_to_all | solution.py:83
  133.1 0.7 fusion.34
  (24 shorter events, 1.4 us)
Async XLA Ops:
  7.2 29.4 %copy-start.1 = (s32[4,128]{1,0:T(4,128)S(1)}, s32[4,128]{1,0:T(4,128)}, u32[]{:S(2)}) copy-start(s32[4,128]{1,0:T(4,128)} %param.5) | copy-start | bytes 6148
  7.2 58.6 %all-gather.2.cloned.1.call-start = ((), (), s32[]{:S(2)}) async-start(), calls=%async_computation.2 | async-start | bytes 1310720 | tf_op jit(solution)/shard_map/all_gather | solution.py:64
  27.4 9.4 %collective-permute-start = (s32[4,128]{1,0:T(4,128)}, s32[4,128]{1,0:T(4,128)S(1)}, u32[]{:S(2)}, u32[]{:S(2)}) collective-permute-start(s32[4,128]{1,0:T(4,128)} %param.5), channel_id=1, source_target_pairs={{0,8},{8,0},{1,9},{9,1},{2,10},{10,2},{3,11},{11,3},{4,12},{12,4},... | collective-permute-start | bytes 6152 | tf_op jit(solution)/shard_map/ppermute | solution.py:68
  65.8 5.8 %copy-start = (bf16[4,128,1024]{2,1,0:T(8,128)(2,1)S(1)}, bf16[4,128,1024]{2,1,0:T(8,128)(2,1)}, u32[]{:S(2)}) copy-start(bf16[4,128,1024]{2,1,0:T(8,128)(2,1)} %all-gather.2.cloned.1.call-done) | copy-start | bytes 3145732
  65.8 9.7 %collective-permute-start.1 = (bf16[4,128,1024]{2,1,0:T(8,128)(2,1)}, bf16[4,128,1024]{2,1,0:T(8,128)(2,1)S(1)}, u32[]{:S(2)}, u32[]{:S(2)}) collective-permute-start(bf16[4,128,1024]{2,1,0:T(8,128)(2,1)} %all-gather.2.cloned.1.call-done), channel_id=1, source_target_pairs={{0,8},{8,0},{1,9},{9,1},{2,10},{10,2},{3,11},{11,3},{4,12},{12,4},... | collective-permute-start | bytes 3145736 | tf_op jit(solution)/shard_map/ppermute | solution.py:67
Sparse Core Ops, SparseCore 0:
  27.5 38.2 all-gather.1

commit v7 on v6

--- a/solution.py
+++ b/solution.py
@@ -61,7 +61,9 @@
 
 def per_device(spectra, pair_list, mask):
     g = lax.all_gather(spectra, "zh", axis=1, tiled=True)
-    g = lax.all_gather(g, "y", axis=1, tiled=True)
+    rep = jnp.broadcast_to(g[None], (4,) + g.shape)
+    got = lax.all_to_all(rep, "y", 0, 0, tiled=True)
+    g = got.transpose(1, 0, 2, 3).reshape(g.shape[0], 4 * g.shape[1], g.shape[2])
     core = lax.axis_index("c")
     swap = [(0, 1), (1, 0)]
     g_other = lax.ppermute(g, "c", swap)

time: 142 us -> 113 us (0.80)
  waiting for transfers between devices: 28.3 us -> 2.56 us
  between operations: 14.3 us -> 0.88 us
  starting transfers between devices: 7.35 us -> 15.1 us
  blocking collectives: 68.3 us -> 72.2 us
  matrix products: 9.6 us -> 7.7 us
    all_gather x1 -> x0, waiting for transfers between devices: 28.3 us -> none  [per_device(): g = lax.all_gather(g, 'y', axis=1, tiled=True)]
    all_to_all x1, blocking collectives: 26.7 us -> 32.7 us  [per_device(): own = lax.all_to_all(p, 'zl', 0, 0, tiled=True).sum(0)]
    all_to_all x0 -> x1, starting transfers between devices: none -> 4.75 us  [per_device(): got = lax.all_to_all(rep, 'y', 0, 0, tiled=True)]
    all_to_all x0 -> x1, waiting for transfers between devices: none -> 2.56 us  [per_device(): got = lax.all_to_all(rep, 'y', 0, 0, tiled=True)]
    all_gather x1, blocking collectives: 20.1 us -> 18 us  [per_device(): g = lax.all_gather(spectra, 'zh', axis=1, tiled=True)]
    ppermute x1, starting transfers between devices: 3.79 us -> 5.84 us  [per_device(): g_other = lax.ppermute(g, 'c', swap)]
where the time goes in v7:
time: 113 us; the launch traced here: 112 us
  blocking collectives  72.2 us (64%)
  starting transfers between devices  15.1 us (13%)
  other arithmetic  10.2 us (9%)
  matrix products  7.7 us (7%)
  local copies, waits for them, and re-layouts  3.09 us (3%)
  waiting for transfers between devices  2.56 us (2%)
    all_to_all x1, blocking collectives, per_device(): own = lax.all_to_all(p, 'zl', 0, 0, tiled=True).sum(0)  32.7 us
    all_to_all x1, blocking collectives, per_device(): lax.all_to_all(packed.reshape(8, 4, -1, cols).transpose(1, 0, 2, 3), 'x',...  21.6 us
    all_gather x1, blocking collectives, per_device(): g = lax.all_gather(spectra, 'zh', axis=1, tiled=True)  18 us
    another operation x3, other arithmetic  6.19 us
    ppermute x1, starting transfers between devices, per_device(): g_other = lax.ppermute(g, 'c', swap)  5.84 us
    all_to_all x1, starting transfers between devices, per_device(): got = lax.all_to_all(rep, 'y', 0, 0, tiled=True)  4.75 us
    ppermute x1, starting transfers between devices, per_device(): mask_other = lax.ppermute(mask, 'c', swap)  4.48 us
    dot_general x2, matrix products, day_sums(): lax.dot_general(cross, table, (((2,), (1,)), ((), ())), preferred_element...  3.83 us
  transfers between devices with their start and end apart: 3, of which 1 were waited for; matrix products, arithmetic and copies ran while one was open for 9% of the time, Pallas kernels for 0%

profile of v7, /device:TPU:1, one launch (start us, length us, event | category | flops | bytes accessed | tf_op | source)
XLA Modules:
  0.0 111.7 jit_solution(4872577481286802254)
XLA Ops:
  0.6 18.0 %all_gather.3 = bf16[4,32,1024]{2,1,0:T(8,128)(2,1)S(1)} all-gather(bf16[4,16,1024]{2,1,0:T(8,128)(2,1)} %param.3), channel_id=1, replica_groups=mesh['x'=4,'zl'=8,'c'=2,'y'=4,'zh'=2] {'zh'}, dimensions={1}, use_global_device_ids=true | all-gather | bytes 393216 | tf_op jit(solution)/shard_map/all_gather | solution.py:63
  18.6 1.1 %broadcast_in_dim.2 = bf16[4,4,32,1024]{3,2,1,0:T(8,128)(2,1)} broadcast(bf16[4,32,1024]{2,1,0:T(8,128)(2,1)S(1)} %all_gather.3), dimensions={1,2,3} | broadcast | bytes 1310720 | tf_op jit(solution)/shard_map/broadcast_in_dim | solution.py:64
  19.7 4.8 %all-to-all-start = ((bf16[4,4,32,1024]{3,2,1,0:T(8,128)(2,1)}), bf16[4,4,32,1024]{3,2,1,0:T(8,128)(2,1)S(1)}, u32[]{:S(2)}, u32[]{:S(2)}) async-start(bf16[4,4,32,1024]{3,2,1,0:T(8,128)(2,1)} %broadcast_in_dim.2), calls=%async_computation | async-start | bytes 2097152 | tf_op jit(solution)/shard_map/all_to_all | solution.py:65
  24.5 4.5 %collective-permute-start = (s32[4,128]{1,0:T(4,128)S(1)}, s32[4,128]{1,0:T(4,128)S(1)}, u32[]{:S(2)}, u32[]{:S(2)}) collective-permute-start(s32[4,128]{1,0:T(4,128)S(1)} %copy-done.1), channel_id=1, source_target_pairs={{0,8},{8,0},{1,9},{9,1},{2,10},{10,2},{3,11},{11,3},{4,12},{12,4},... | collective-permute-start | bytes 6152 | tf_op jit(solution)/shard_map/ppermute | solution.py:70
  29.3 3.7 %negate_convert_fusion = (bf16[401,512]{1,0:T(8,128)(2,1)S(1)}, bf16[401,512]{1,0:T(8,128)(2,1)S(1)}, bf16[401,512]{1,0:T(8,128)(2,1)S(1)}) fusion(s32[401]{0:T(512)S(1)} %iota_add_fusion), kind=kLoop, calls=%fused_computation.33 | loop fusion | flops 4106240 | bytes 1233476 | tf_op jit(solution)/shard_map/convert.7
  33.1 0.2 fusion.16
  33.3 0.2 fusion.43
  33.5 0.2 fusion.15
  33.8 0.2 fusion.44
  34.2 2.6 %all-to-all-done = bf16[4,4,32,1024]{3,2,1,0:T(8,128)(2,1)S(1)} async-done(((bf16[4,4,32,1024]{3,2,1,0:T(8,128)(2,1)}), bf16[4,4,32,1024]{3,2,1,0:T(8,128)(2,1)S(1)}, u32[]{:S(2)}, u32[]{:S(2)}) %all-to-all-start) | async-done | bytes 1048608 | tf_op jit(solution)/shard_map/all_to_all | solution.py:65
  36.9 5.8 %collective-permute-start.1 = (bf16[4,128,1024]{2,1,0:T(8,128)(2,1)S(1)}, bf16[4,128,1024]{2,1,0:T(8,128)(2,1)S(1)}, u32[]{:S(2)}, u32[]{:S(2)}) collective-permute-start(bf16[4,128,1024]{2,1,0:T(8,128)(2,1)S(1)} %bitcast.47), channel_id=1, source_target_pairs={{0,8},{8,0},{1,9},{9,1},{2,10},{10,2},{3,11},{11,3},{4,12},{12,4},... | collective-permute-start | bytes 3145736 | tf_op jit(solution)/shard_map/ppermute | solution.py:69
  42.7 0.7 convolution_bitcast_fusion.2
  43.4 0.7 convolution_bitcast_fusion.3
  44.2 1.2 %add_convert_fusion.1 = (bf16[4,256,512]{2,1,0:T(8,128)(2,1)S(1)}, bf16[4,256,512]{2,1,0:T(8,128)(2,1)S(1)}) fusion(f32[4,256,1024]{2,1,0:T(8,128)S(1)} %convolution_bitcast_fusion.2, f32[4,256,1024]{2,1,0:T(8,128)S(1)} %convolution_bitcast_fusion.3), kind=kLoop, calls=%fused_computation.15 | loop fusion | flops 4194304 | bytes 10485760 | tf_op jit(solution)/shard_map/convert.8
  45.4 1.9 %fusion = f32[4,256,802]{1,2,0:T(8,128)S(1)} fusion(bf16[4,256,512]{2,1,0:T(8,128)(2,1)S(1)} %get-tuple-element.13, bf16[4,256,512]{2,1,0:T(8,128)(2,1)S(1)} %get-tuple-element.12, bf16[401,512]{1,0:T(8,128)(2,1)S(1)} %get-tuple-element.18, bf16[401,512]{1,0:T(8,128)(2,1)S(1)} %get-tuple-element.17, bf16[401,512]{1,0:T(8,128)(2,1)S(1)} %get-tuple-element.16), kind=kOutput, calls=%fused_computation.4 | convolution fusion | flops 1692680192 | bytes 6614016 | tf_op jit(solution)/shard_map/dot_general | solution.py:48
  47.3 0.7 convolution_bitcast_fusion.1
  48.1 0.7 convolution_bitcast_fusion
  48.8 1.2 %add_convert_fusion = (bf16[4,256,512]{2,1,0:T(8,128)(2,1)S(1)}, bf16[4,256,512]{2,1,0:T(8,128)(2,1)S(1)}) fusion(f32[4,256,1024]{2,1,0:T(8,128)S(1)} %convolution_bitcast_fusion, f32[4,256,1024]{2,1,0:T(8,128)S(1)} %convolution_bitcast_fusion.1), kind=kLoop, calls=%fused_computation.13 | loop fusion | flops 4194304 | bytes 10485760 | tf_op jit(solution)/shard_map/convert
  50.1 1.9 %fusion.4 = f32[4,256,802]{1,2,0:T(8,128)S(1)} fusion(bf16[4,256,512]{2,1,0:T(8,128)(2,1)S(1)} %get-tuple-element.11, bf16[4,256,512]{2,1,0:T(8,128)(2,1)S(1)} %get-tuple-element.10, bf16[401,512]{1,0:T(8,128)(2,1)S(1)} %get-tuple-element.18, bf16[401,512]{1,0:T(8,128)(2,1)S(1)} %get-tuple-element.17, bf16[401,512]{1,0:T(8,128)(2,1)S(1)} %get-tuple-element.16), kind=kOutput, calls=%fused_computation.8 | convolution fusion | flops 1692680192 | bytes 6614016 | tf_op jit(solution)/shard_map/dot_general | solution.py:48
  52.0 2.8 %multiply_reduce_fusion = (f32[256,401]{0,1:T(8,128)S(1)}, f32[256,401]{0,1:T(8,128)S(1)}, f32[256,401]{0,1:T(8,128)S(1)}, f32[256,401]{0,1:T(8,128)S(1)}, f32[256,401]{0,1:T(8,128)S(1)}, /*index=5*/f32[256,401]{0,1:T(8,128)S(1)}) fusion(f32[4,256,802]{1,2,0:T(8,128)S(1)} %fusion.4, f32[4,256]{1,0:T(4,128)S(1)} %bitcast.65, f32[4,256,802]{1,2,0:T(8,128)S(1)} %fusion, ...), kind=kLoop, calls=%fused_computation.16 | loop fusion | flops 10060288 | bytes 9041920 | tf_op jit(solution)/shard_map/reduce_sum | solution.py:58
  55.6 0.7 concatenate.29
  56.4 21.6 %all_to_all.15 = f32[4,8,8,1204]{3,2,1,0:T(8,128)S(1)} all-to-all(f32[4,8,8,1204]{3,2,1,0:T(8,128)S(1)} %copy.26), channel_id=1, replica_groups=mesh['x'=4,'zl'=8,'c'=2,'y'=4,'zh'=2] {'x'}, dimensions={0} | all-to-all | bytes 2465792 | tf_op jit(solution)/shard_map/all_to_all | solution.py:84
  78.1 32.7 %all_to_all.16 = f32[8,8,1204]{2,1,0:T(8,128)S(1)} all-to-all(f32[8,8,1204]{2,1,0:T(8,128)S(1)} %reduce_sum.98), channel_id=1, replica_groups=mesh['x'=4,'zl'=8,'c'=2,'y'=4,'zh'=2] {'zl'}, dimensions={0} | all-to-all | bytes 616448 | tf_op jit(solution)/shard_map/all_to_all | solution.py:85
  111.0 0.7 fusion.34
  (25 shorter events, 1.7 us)
Async XLA Ops:
  0.6 23.8 %copy-start.1 = (s32[4,128]{1,0:T(4,128)S(1)}, s32[4,128]{1,0:T(4,128)}, u32[]{:S(2)}) copy-start(s32[4,128]{1,0:T(4,128)} %param.5) | copy-start | bytes 6148
  0.6 28.4 %copy-start = (s32[512,2]{0,1:T(2,128)S(1)}, s32[512,2]{0,1:T(2,128)}, u32[]{:S(2)}) copy-start(s32[512,2]{0,1:T(2,128)} %param.4) | copy-start | bytes 12292
  19.7 17.1 %all-to-all-start = ((bf16[4,4,32,1024]{3,2,1,0:T(8,128)(2,1)}), bf16[4,4,32,1024]{3,2,1,0:T(8,128)(2,1)S(1)}, u32[]{:S(2)}, u32[]{:S(2)}) async-start(bf16[4,4,32,1024]{3,2,1,0:T(8,128)(2,1)} %broadcast_in_dim.2), calls=%async_computation | async-start | bytes 2097152 | tf_op jit(solution)/shard_map/all_to_all | solution.py:65
  24.5 9.1 %collective-permute-start = (s32[4,128]{1,0:T(4,128)S(1)}, s32[4,128]{1,0:T(4,128)S(1)}, u32[]{:S(2)}, u32[]{:S(2)}) collective-permute-start(s32[4,128]{1,0:T(4,128)S(1)} %copy-done.1), channel_id=1, source_target_pairs={{0,8},{8,0},{1,9},{9,1},{2,10},{10,2},{3,11},{11,3},{4,12},{12,4},... | collective-permute-start | bytes 6152 | tf_op jit(solution)/shard_map/ppermute | solution.py:70
  36.9 10.5 %collective-permute-start.1 = (bf16[4,128,1024]{2,1,0:T(8,128)(2,1)S(1)}, bf16[4,128,1024]{2,1,0:T(8,128)(2,1)S(1)}, u32[]{:S(2)}, u32[]{:S(2)}) collective-permute-start(bf16[4,128,1024]{2,1,0:T(8,128)(2,1)S(1)} %bitcast.47), channel_id=1, source_target_pairs={{0,8},{8,0},{1,9},{9,1},{2,10},{10,2},{3,11},{11,3},{4,12},{12,4},... | collective-permute-start | bytes 3145736 | tf_op jit(solution)/shard_map/ppermute | solution.py:69

commit v8 on v7

--- a/solution.py
+++ b/solution.py
@@ -72,21 +72,23 @@
     k = pair_list.shape[0] // (nx * nz * nc)
     pl = pair_list.reshape(nx, nz, nc, k, 2)
     pl = lax.dynamic_index_in_dim(pl, core, 2, keepdims=False)
-    pl = pl.transpose(1, 0, 2, 3).reshape(nz * nx * k, 2)
+    pl = pl.reshape(nx * nz * k, 2)
     first = pl[:, 0]
     second = pl[:, 1]
     table = lag_table()
     mine = day_sums(g, mask, first, second, table)
     theirs = day_sums(g_other, mask_other, first, second, table)
     sums = [a + b for a, b in zip(mine, theirs)]
-    packed = jnp.concatenate(list(sums), 1)
+    width = sum(x.shape[1] for x in sums)
+    pad = jnp.zeros((sums[0].shape[0], -width % 128), jnp.float32)
+    packed = jnp.concatenate(list(sums) + [pad], 1)
     cols = packed.shape[1]
-    p = lax.all_to_all(packed.reshape(8, 4, -1, cols).transpose(1, 0, 2, 3), "x", 0, 0, tiled=True).sum(0)
+    p = lax.all_to_all(packed.reshape(4, 8, -1, cols), "x", 0, 0, tiled=True).sum(0)
     own = lax.all_to_all(p, "zl", 0, 0, tiled=True).sum(0)
     lin_own = own[:, :LAGS]
     real_own = own[:, LAGS : 2 * LAGS]
     imag_own = own[:, 2 * LAGS : 3 * LAGS]
-    count_own = own[:, 3 * LAGS :]
+    count_own = own[:, 3 * LAGS : 3 * LAGS + 1]
     linear_stack = lin_own / count_own
     weighted_stack = (
         linear_stack * (real_own * real_own + imag_own * imag_own) / (count_own * count_own)

time: 113 us -> 113 us (level)
  no operation moved by 1% of the time
where the time goes in v8:
time: 113 us; the launch traced here: 112 us
  blocking collectives  72.2 us (64%)
  starting transfers between devices  15.1 us (13%)
  other arithmetic  10.2 us (9%)
  matrix products  7.7 us (7%)
  local copies, waits for them, and re-layouts  3.11 us (3%)
  waiting for transfers between devices  2.52 us (2%)
    all_to_all x1, blocking collectives, per_device(): own = lax.all_to_all(p, 'zl', 0, 0, tiled=True).sum(0)  32.7 us
    all_to_all x1, blocking collectives, per_device(): lax.all_to_all(packed.reshape(4, 8, -1, cols), 'x', 0, 0, tiled=True).sum(0)  21.6 us
    all_gather x1, blocking collectives, per_device(): g = lax.all_gather(spectra, 'zh', axis=1, tiled=True)  18 us
    another operation x3, other arithmetic  6.19 us
    ppermute x1, starting transfers between devices, per_device(): g_other = lax.ppermute(g, 'c', swap)  5.84 us
    all_to_all x1, starting transfers between devices, per_device(): got = lax.all_to_all(rep, 'y', 0, 0, tiled=True)  4.75 us
    ppermute x1, starting transfers between devices, per_device(): mask_other = lax.ppermute(mask, 'c', swap)  4.48 us
    dot_general x2, matrix products, day_sums(): lax.dot_general(cross, table, (((2,), (1,)), ((), ())), preferred_element...  3.83 us
  transfers between devices with their start and end apart: 3, of which 1 were waited for; matrix products, arithmetic and copies ran while one was open for 9% of the time, Pallas kernels for 0%

profile of v8, /device:TPU:1, one launch (start us, length us, event | category | flops | bytes accessed | tf_op | source)
XLA Modules:
  0.0 111.6 jit_solution(16139837467937776547)
XLA Ops:
  0.6 18.0 %all_gather.3 = bf16[4,32,1024]{2,1,0:T(8,128)(2,1)S(1)} all-gather(bf16[4,16,1024]{2,1,0:T(8,128)(2,1)} %param.3), channel_id=1, replica_groups=mesh['x'=4,'zl'=8,'c'=2,'y'=4,'zh'=2] {'zh'}, dimensions={1}, use_global_device_ids=true | all-gather | bytes 393216 | tf_op jit(solution)/shard_map/all_gather | solution.py:63
  18.6 1.1 %broadcast_in_dim.4 = bf16[4,4,32,1024]{3,2,1,0:T(8,128)(2,1)} broadcast(bf16[4,32,1024]{2,1,0:T(8,128)(2,1)S(1)} %all_gather.3), dimensions={1,2,3} | broadcast | bytes 1310720 | tf_op jit(solution)/shard_map/broadcast_in_dim | solution.py:64
  19.7 4.8 %all-to-all-start = ((bf16[4,4,32,1024]{3,2,1,0:T(8,128)(2,1)}), bf16[4,4,32,1024]{3,2,1,0:T(8,128)(2,1)S(1)}, u32[]{:S(2)}, u32[]{:S(2)}) async-start(bf16[4,4,32,1024]{3,2,1,0:T(8,128)(2,1)} %broadcast_in_dim.4), calls=%async_computation | async-start | bytes 2097152 | tf_op jit(solution)/shard_map/all_to_all | solution.py:65
  24.5 4.5 %collective-permute-start = (s32[4,128]{1,0:T(4,128)S(1)}, s32[4,128]{1,0:T(4,128)S(1)}, u32[]{:S(2)}, u32[]{:S(2)}) collective-permute-start(s32[4,128]{1,0:T(4,128)S(1)} %copy-done.1), channel_id=1, source_target_pairs={{0,8},{8,0},{1,9},{9,1},{2,10},{10,2},{3,11},{11,3},{4,12},{12,4},... | collective-permute-start | bytes 6152 | tf_op jit(solution)/shard_map/ppermute | solution.py:70
  29.4 3.7 %negate_convert_fusion = (bf16[401,512]{1,0:T(8,128)(2,1)S(1)}, bf16[401,512]{1,0:T(8,128)(2,1)S(1)}, bf16[401,512]{1,0:T(8,128)(2,1)S(1)}) fusion(s32[401]{0:T(512)S(1)} %iota_add_fusion), kind=kLoop, calls=%fused_computation.33 | loop fusion | flops 4106240 | bytes 1233476 | tf_op jit(solution)/shard_map/convert.7
  33.1 0.2 fusion.16
  33.3 0.2 fusion.43
  33.6 0.2 fusion.15
  33.8 0.2 fusion.44
  34.3 2.5 %all-to-all-done = bf16[4,4,32,1024]{3,2,1,0:T(8,128)(2,1)S(1)} async-done(((bf16[4,4,32,1024]{3,2,1,0:T(8,128)(2,1)}), bf16[4,4,32,1024]{3,2,1,0:T(8,128)(2,1)S(1)}, u32[]{:S(2)}, u32[]{:S(2)}) %all-to-all-start) | async-done | bytes 1048608 | tf_op jit(solution)/shard_map/all_to_all | solution.py:65
  36.9 5.8 %collective-permute-start.1 = (bf16[4,128,1024]{2,1,0:T(8,128)(2,1)S(1)}, bf16[4,128,1024]{2,1,0:T(8,128)(2,1)S(1)}, u32[]{:S(2)}, u32[]{:S(2)}) collective-permute-start(bf16[4,128,1024]{2,1,0:T(8,128)(2,1)S(1)} %bitcast.43), channel_id=1, source_target_pairs={{0,8},{8,0},{1,9},{9,1},{2,10},{10,2},{3,11},{11,3},{4,12},{12,4},... | collective-permute-start | bytes 3145736 | tf_op jit(solution)/shard_map/ppermute | solution.py:69
  42.7 0.7 convolution_bitcast_fusion.2
  43.4 0.7 convolution_bitcast_fusion.3
  44.2 1.2 %add_convert_fusion.1 = (bf16[4,256,512]{2,1,0:T(8,128)(2,1)S(1)}, bf16[4,256,512]{2,1,0:T(8,128)(2,1)S(1)}) fusion(f32[4,256,1024]{2,1,0:T(8,128)S(1)} %convolution_bitcast_fusion.2, f32[4,256,1024]{2,1,0:T(8,128)S(1)} %convolution_bitcast_fusion.3), kind=kLoop, calls=%fused_computation.15 | loop fusion | flops 4194304 | bytes 10485760 | tf_op jit(solution)/shard_map/convert.8
  45.4 1.9 %fusion = f32[4,256,802]{1,2,0:T(8,128)S(1)} fusion(bf16[4,256,512]{2,1,0:T(8,128)(2,1)S(1)} %get-tuple-element.13, bf16[4,256,512]{2,1,0:T(8,128)(2,1)S(1)} %get-tuple-element.12, bf16[401,512]{1,0:T(8,128)(2,1)S(1)} %get-tuple-element.18, bf16[401,512]{1,0:T(8,128)(2,1)S(1)} %get-tuple-element.17, bf16[401,512]{1,0:T(8,128)(2,1)S(1)} %get-tuple-element.16), kind=kOutput, calls=%fused_computation.4 | convolution fusion | flops 1692680192 | bytes 6614016 | tf_op jit(solution)/shard_map/dot_general | solution.py:48
  47.3 0.7 convolution_bitcast_fusion.1
  48.1 0.7 convolution_bitcast_fusion
  48.8 1.2 %add_convert_fusion = (bf16[4,256,512]{2,1,0:T(8,128)(2,1)S(1)}, bf16[4,256,512]{2,1,0:T(8,128)(2,1)S(1)}) fusion(f32[4,256,1024]{2,1,0:T(8,128)S(1)} %convolution_bitcast_fusion, f32[4,256,1024]{2,1,0:T(8,128)S(1)} %convolution_bitcast_fusion.1), kind=kLoop, calls=%fused_computation.13 | loop fusion | flops 4194304 | bytes 10485760 | tf_op jit(solution)/shard_map/convert
  50.1 1.9 %fusion.4 = f32[4,256,802]{1,2,0:T(8,128)S(1)} fusion(bf16[4,256,512]{2,1,0:T(8,128)(2,1)S(1)} %get-tuple-element.11, bf16[4,256,512]{2,1,0:T(8,128)(2,1)S(1)} %get-tuple-element.10, bf16[401,512]{1,0:T(8,128)(2,1)S(1)} %get-tuple-element.18, bf16[401,512]{1,0:T(8,128)(2,1)S(1)} %get-tuple-element.17, bf16[401,512]{1,0:T(8,128)(2,1)S(1)} %get-tuple-element.16), kind=kOutput, calls=%fused_computation.8 | convolution fusion | flops 1692680192 | bytes 6614016 | tf_op jit(solution)/shard_map/dot_general | solution.py:48
  52.0 2.8 %multiply_reduce_fusion = (f32[256,401]{0,1:T(8,128)S(1)}, f32[256,401]{0,1:T(8,128)S(1)}, f32[256,401]{0,1:T(8,128)S(1)}, f32[256,401]{0,1:T(8,128)S(1)}, f32[256,401]{0,1:T(8,128)S(1)}, /*index=5*/f32[256,401]{0,1:T(8,128)S(1)}) fusion(f32[4,256,802]{1,2,0:T(8,128)S(1)} %fusion.4, f32[4,256]{1,0:T(4,128)S(1)} %bitcast.59, f32[4,256,802]{1,2,0:T(8,128)S(1)} %fusion, ...), kind=kLoop, calls=%fused_computation.16 | loop fusion | flops 10060288 | bytes 9041920 | tf_op jit(solution)/shard_map/reduce_sum | solution.py:58
  55.6 0.8 concatenate.29
  56.4 21.6 %all_to_all.15 = f32[4,8,8,1280]{3,2,1,0:T(8,128)S(1)} all-to-all(f32[4,8,8,1280]{3,2,1,0:T(8,128)S(1)} %concatenate.29), channel_id=1, replica_groups=mesh['x'=4,'zl'=8,'c'=2,'y'=4,'zh'=2] {'x'}, dimensions={0} | all-to-all | bytes 2621440 | tf_op jit(solution)/shard_map/all_to_all | solution.py:86
  78.0 32.7 %all_to_all.16 = f32[8,8,1280]{2,1,0:T(8,128)S(1)} all-to-all(f32[8,8,1280]{2,1,0:T(8,128)S(1)} %reduce_sum.98), channel_id=1, replica_groups=mesh['x'=4,'zl'=8,'c'=2,'y'=4,'zh'=2] {'zl'}, dimensions={0} | all-to-all | bytes 655360 | tf_op jit(solution)/shard_map/all_to_all | solution.py:87
  111.0 0.7 fusion.34
  (24 shorter events, 1.7 us)
Async XLA Ops:
  0.6 23.8 %copy-start.1 = (s32[4,128]{1,0:T(4,128)S(1)}, s32[4,128]{1,0:T(4,128)}, u32[]{:S(2)}) copy-start(s32[4,128]{1,0:T(4,128)} %param.5) | copy-start | bytes 6148
  0.6 28.4 %copy-start = (s32[512,2]{0,1:T(2,128)S(1)}, s32[512,2]{0,1:T(2,128)}, u32[]{:S(2)}) copy-start(s32[512,2]{0,1:T(2,128)} %param.4) | copy-start | bytes 12292
  19.7 17.1 %all-to-all-start = ((bf16[4,4,32,1024]{3,2,1,0:T(8,128)(2,1)}), bf16[4,4,32,1024]{3,2,1,0:T(8,128)(2,1)S(1)}, u32[]{:S(2)}, u32[]{:S(2)}) async-start(bf16[4,4,32,1024]{3,2,1,0:T(8,128)(2,1)} %broadcast_in_dim.4), calls=%async_computation | async-start | bytes 2097152 | tf_op jit(solution)/shard_map/all_to_all | solution.py:65
  24.5 9.1 %collective-permute-start = (s32[4,128]{1,0:T(4,128)S(1)}, s32[4,128]{1,0:T(4,128)S(1)}, u32[]{:S(2)}, u32[]{:S(2)}) collective-permute-start(s32[4,128]{1,0:T(4,128)S(1)} %copy-done.1), channel_id=1, source_target_pairs={{0,8},{8,0},{1,9},{9,1},{2,10},{10,2},{3,11},{11,3},{4,12},{12,4},... | collective-permute-start | bytes 6152 | tf_op jit(solution)/shard_map/ppermute | solution.py:70
  36.9 10.5 %collective-permute-start.1 = (bf16[4,128,1024]{2,1,0:T(8,128)(2,1)S(1)}, bf16[4,128,1024]{2,1,0:T(8,128)(2,1)S(1)}, u32[]{:S(2)}, u32[]{:S(2)}) collective-permute-start(bf16[4,128,1024]{2,1,0:T(8,128)(2,1)S(1)} %bitcast.43), channel_id=1, source_target_pairs={{0,8},{8,0},{1,9},{9,1},{2,10},{10,2},{3,11},{11,3},{4,12},{12,4},... | collective-permute-start | bytes 3145736 | tf_op jit(solution)/shard_map/ppermute | solution.py:69
